TPU v7x, 128 devices: a whole 4x4x4 slice. The times are simulated.
128 devices in a mesh: pool: 4 (over x_hi, core), grp: 4 (over y), tp: 8 (over z, x_lo).
Axes of the slice: x: 4 (x_hi: 2, x_lo: 2; x = x_hi * 2 + x_lo), y: 4, z: 4, core: 2. Of those that a mesh axis runs over, the one named last changes fastest.
Arguments:
- hidden: bfloat16 [1024, 8192], P('pool', 'grp'), may hold values from -6 to 6
- attn_gain: float32 [8192], P('grp'), may hold values from 0.25 to 1.75
- w_query: bfloat16 [8192, 8192], P('grp', 'tp'), may hold values from -0.0625 to 0.0625
- w_key: bfloat16 [8192, 1024], P('grp', 'tp'), may hold values from -1 to 1
- w_value: bfloat16 [8192, 1024], P('grp', 'tp'), may hold values from -0.0625 to 0.0625
- w_out: bfloat16 [8192, 8192], P('tp', 'grp'), may hold values from -0.0625 to 0.0625
- prefix_keys: bfloat16 [8, 16384, 1024], P('pool', 'grp', 'tp'), may hold values from -300 to 300
- prefix_values: bfloat16 [8, 16384, 1024], P('pool', 'grp', 'tp'), may hold values from -6 to 6
- suffix_keys: bfloat16 [1024, 256, 1024], P('pool', 'grp', 'tp'), may hold values from -300 to 300
- suffix_values: bfloat16 [1024, 256, 1024], P('pool', 'grp', 'tp'), may hold values from -6 to 6
- prefix_ids: int32 [1024], P('pool'), may hold values from 0 to 7, as said below
- suffix_lens: int32 [1024], P('pool'), may hold values from 1 to 256, as said below
- ffn_gain: float32 [8192], P('grp'), may hold values from 0.25 to 1.75
- w_gate: bfloat16 [8192, 14336], P('grp', ('pool', 'tp')), may hold values from -0.0625 to 0.0625
- w_up: bfloat16 [8192, 14336], P('grp', ('pool', 'tp')), may hold values from -0.0625 to 0.0625
- w_down: bfloat16 [14336, 8192], P(('pool', 'tp'), 'grp'), may hold values from -0.046875 to 0.046875
Outputs:
- result: bfloat16 [1024, 8192], P(('pool', 'tp'), 'grp')
Inputs may be any that keep to these rules, and one draw needn't show every extreme that they name: `prefix_ids`: within rows p * 256 to (p + 1) * 256 - 1, each of the prefixes p * 2 to (p + 1) * 2 - 1 is named by exactly 128 streams, and no other prefix is named. `suffix_lens`: each block of 256 streams holds a stream of length 256 and one of length 1.
All inputs are finite; a program needn't handle non-finite values.
Results may differ from a plain program's by a relative error of at most 0.015.
Values may be sent and summed in bfloat16 or wider, within the bound.
No kernel may reach another device: no remote copies, remote signals or barrier semaphores. Data moves between devices by JAX's collectives and lax.ppermute only.
A program may use at most 192 MiB of HBM per device.

v0:
```python
import math

import jax
import jax.numpy as jnp
from jax import lax
from jax.sharding import PartitionSpec as P

D = 8192
HD = 128
TP = ("z", "xlo")


epsilon = 1e-05


def joined(array, axis, combine):
    everything = jax.tree.map(lambda part: lax.all_gather(part, axis), array)
    first = jax.tree.map(lambda part: part[0], everything)

    def lap(k, so_far):
        return combine(so_far, jax.tree.map(lambda part: part[k], everything))

    return lax.fori_loop(1, lax.axis_size(axis), lap, first)


def combine_parts(earlier, later):
    peak_one, total_one, numer_one = earlier
    peak_two, total_two, numer_two = later
    peak = jnp.maximum(peak_one, peak_two)
    scale_one = jnp.exp(peak_one - peak)
    scale_two = jnp.exp(peak_two - peak)
    total = total_one * scale_one + total_two * scale_two
    numer = numer_one * scale_one[..., None] + numer_two * scale_two[..., None]
    return (peak, total, numer)


def pair_gather(part, axis):
    swap = [(0, 1), (1, 0)]
    other = lax.ppermute(part, axis, swap)
    first = lax.axis_index(axis) == 0
    return jnp.where(
        first, jnp.concatenate([part, other], axis=0), jnp.concatenate([other, part], axis=0)
    )


def pair_reduce(rows, axis):
    swap = [(0, 1), (1, 0)]
    index = lax.axis_index(axis)
    halves = rows.reshape((2, rows.shape[0] // 2) + rows.shape[1:])
    mine = lax.dynamic_index_in_dim(halves, index, 0, keepdims=False)
    other = lax.dynamic_index_in_dim(halves, 1 - index, 0, keepdims=False)
    other = lax.ppermute(other.astype(jnp.bfloat16), axis, swap)
    return mine.astype(jnp.float32) + other.astype(jnp.float32)


def ring_gather(part, axis):
    size = lax.axis_size(axis)
    index = lax.axis_index(axis)
    pieces = [part]
    for shift in range(1, size):
        pairs = [(i, (i + shift) % size) for i in range(size)]
        pieces.append(lax.ppermute(part, axis, pairs))
    stacked = jnp.stack(pieces)
    order = (index - jnp.arange(size, dtype=jnp.int32)) % size
    return stacked[order].reshape((size * part.shape[0],) + part.shape[1:])


def ring_reduce(rows, axis):
    size = lax.axis_size(axis)
    index = lax.axis_index(axis)
    blocks = rows.reshape((size, rows.shape[0] // size) + rows.shape[1:])
    total = lax.dynamic_index_in_dim(blocks, index, 0, keepdims=False).astype(jnp.float32)
    for shift in range(1, size):
        pairs = [(i, (i + shift) % size) for i in range(size)]
        outgoing = lax.dynamic_index_in_dim(blocks, (index + shift) % size, 0, keepdims=False)
        total = total + lax.ppermute(outgoing, axis, pairs).astype(jnp.float32)
    return total


def small_reduce(value, axis, combine):
    return combine(ring_gather(value[None], axis), axis=0)


def body(
    hidden,
    attn_gain,
    w_query,
    w_key,
    w_value,
    w_out,
    prefix_keys,
    prefix_values,
    suffix_keys,
    suffix_values,
    prefix_ids,
    suffix_lens,
    ffn_gain,
    w_gate,
    w_up,
    w_down,
):
    stream_count = hidden.shape[0]
    hidden_float = hidden.astype(jnp.float32)
    squares = small_reduce(jnp.sum(hidden_float * hidden_float, axis=1), "grp", jnp.sum)
    inverse = lax.rsqrt(squares / D + epsilon)
    normed = (hidden_float * inverse[:, None] * attn_gain).astype(jnp.bfloat16)
    part_query = jnp.dot(normed, w_query, preferred_element_type=jnp.float32)
    part_key = jnp.dot(normed, w_key, preferred_element_type=jnp.float32)
    part_value = jnp.dot(normed, w_value, preferred_element_type=jnp.float32)
    projected = jnp.concatenate([part_query, part_key, part_value], axis=1)
    projected = ring_gather(ring_reduce(projected, "grp").astype(jnp.bfloat16), "grp")
    q_width = part_query.shape[1]
    k_width = part_key.shape[1]
    query = projected[:, :q_width]
    key_new = projected[:, q_width : q_width + k_width]
    value_new = projected[:, q_width + k_width :]
    kv_local = w_key.shape[1] // HD
    q_local = w_query.shape[1] // HD
    groups = q_local // kv_local
    prefix_local = prefix_keys.shape[0]
    pre_length = prefix_keys.shape[1]
    suf_length = suffix_keys.shape[1]
    factor = 1.0 / math.sqrt(HD)
    heads = query.reshape(stream_count, kv_local, groups, HD)
    pre_key = prefix_keys.reshape(prefix_local, pre_length, kv_local, HD)
    pre_value = prefix_values.reshape(prefix_local, pre_length, kv_local, HD)
    suf_key = suffix_keys.reshape(stream_count, suf_length, kv_local, HD)
    suf_value = suffix_values.reshape(stream_count, suf_length, kv_local, HD)
    pool_index = lax.axis_index("hi") * lax.axis_size("core") + lax.axis_index("core")
    local_prefix = prefix_ids - pool_index * prefix_local
    per_group = stream_count // prefix_local
    one_hot = (local_prefix[:, None] == jnp.arange(prefix_local, dtype=jnp.int32)[None, :]).astype(
        jnp.int32
    )
    rank_within = jnp.sum(jnp.cumsum(one_hot, axis=0) * one_hot, axis=1) - 1
    target = local_prefix * per_group + rank_within
    group_order = (
        jnp.zeros((stream_count,), jnp.int32)
        .at[target]
        .set(jnp.arange(stream_count, dtype=jnp.int32))
    )
    grouped = heads[group_order].reshape(prefix_local, per_group, kv_local, groups, HD)
    pre_scores = (
        jnp.einsum("pskgd,pjkd->pskgj", grouped, pre_key, preferred_element_type=jnp.float32)
        * factor
    )
    pre_peak = pre_scores.max(axis=4).reshape(stream_count, kv_local, groups)[target]
    positions = lax.axis_index("grp") * suf_length + jnp.arange(suf_length, dtype=jnp.int32)
    valid = (positions[None, :] < suffix_lens[:, None])[:, None, None, :]
    suf_scores = (
        jnp.einsum("skgd,sjkd->skgj", heads, suf_key, preferred_element_type=jnp.float32) * factor
    )
    suf_scores = jnp.where(valid, suf_scores, -1e30)
    own_score = (
        jnp.einsum(
            "skgd,skd->skg",
            heads,
            key_new.reshape(stream_count, kv_local, HD),
            preferred_element_type=jnp.float32,
        )
        * factor
    )
    peak = jnp.maximum(jnp.maximum(pre_peak, suf_scores.max(axis=3)), own_score)
    peak = small_reduce(peak, "grp", jnp.max)
    peak_grouped = peak[group_order].reshape(prefix_local, per_group, kv_local, groups)
    pre_weights = jnp.exp(pre_scores - peak_grouped[..., None]).astype(jnp.bfloat16)
    unit = jnp.zeros((HD,), pre_value.dtype).at[0].set(1)
    pre_value_ext = jnp.concatenate(
        [pre_value, jnp.broadcast_to(unit, pre_value.shape)], axis=3
    )
    pre_both = jnp.einsum(
        "pskgj,pjkd->pskgd", pre_weights, pre_value_ext, preferred_element_type=jnp.float32
    )
    pre_both = pre_both.reshape(stream_count, kv_local, groups, 2 * HD)[target]
    suf_weights = jnp.where(valid, jnp.exp(suf_scores - peak[:, :, :, None]), 0.0).astype(
        jnp.bfloat16
    )
    total = pre_both[..., HD] + suf_weights.astype(jnp.float32).sum(axis=3)
    numer = pre_both[..., :HD] + jnp.einsum(
        "skgj,sjkd->skgd", suf_weights, suf_value, preferred_element_type=jnp.float32
    )
    flat = stream_count, kv_local * groups
    packed = jnp.concatenate([numer.reshape(stream_count, -1), total.reshape(flat)], axis=1)
    reduced = ring_reduce(packed, "grp")
    quarter = reduced.shape[0]
    q_start = lax.axis_index("grp") * quarter
    width = kv_local * groups * HD
    numer = reduced[:, :width].reshape(quarter, kv_local, groups, HD)
    total = reduced[:, width:].reshape(quarter, kv_local, groups)
    own_score = lax.dynamic_slice_in_dim(own_score, q_start, quarter, 0)
    own_peak = lax.dynamic_slice_in_dim(peak, q_start, quarter, 0)
    own_weight = jnp.exp(own_score - own_peak).astype(jnp.bfloat16).astype(jnp.float32)
    total = total + own_weight
    own_value = lax.dynamic_slice_in_dim(value_new, q_start, quarter, 0)
    own_value = own_value.reshape(quarter, kv_local, 1, HD).astype(jnp.float32)
    numer = numer + own_weight[..., None] * own_value
    attended = (numer / total[..., None]).reshape(quarter, q_local * HD).astype(jnp.bfloat16)
    attended = ring_gather(attended, "grp")
    partial_out = jnp.dot(attended, w_out, preferred_element_type=jnp.float32)
    share = stream_count // (lax.axis_size("z") * lax.axis_size("xlo"))
    tp_start = (lax.axis_index("z") * lax.axis_size("xlo") + lax.axis_index("xlo")) * share
    summed = ring_reduce(partial_out.astype(jnp.bfloat16), "z")
    summed = pair_reduce(summed, "xlo")
    own_hidden = lax.dynamic_slice_in_dim(hidden_float, tp_start, share, 0)
    middle = (own_hidden + summed.astype(jnp.float32)).astype(jnp.bfloat16)
    middle_float = middle.astype(jnp.float32)
    ffn_squares = small_reduce(jnp.sum(middle_float * middle_float, axis=1), "grp", jnp.sum)
    ffn_inverse = lax.rsqrt(ffn_squares / D + epsilon)
    normed_own = (middle_float * ffn_inverse[:, None] * ffn_gain).astype(jnp.bfloat16)
    swap = [(0, 1), (1, 0)]
    gate_both = jnp.concatenate([w_gate, lax.ppermute(w_gate, "core", swap)], axis=1)
    up_both = jnp.concatenate([w_up, lax.ppermute(w_up, "core", swap)], axis=1)
    down_both = jnp.concatenate([w_down, lax.ppermute(w_down, "core", swap)], axis=0)
    normed_row = pair_gather(pair_gather(normed_own, "xlo"), "hi")
    normed_half = ring_gather(normed_row, "z")
    hidden_units = gate_both.shape[1]
    part_gate = jnp.dot(normed_half, gate_both, preferred_element_type=jnp.float32)
    part_upward = jnp.dot(normed_half, up_both, preferred_element_type=jnp.float32)
    both = jnp.concatenate([part_gate, part_upward], axis=1).astype(jnp.bfloat16)
    reduced = ring_reduce(both, "grp")
    gate = reduced[:, :hidden_units]
    upward = reduced[:, hidden_units:]
    act = (jax.nn.silu(gate) * upward).astype(jnp.bfloat16)
    act_all = ring_gather(act, "grp")
    down = jnp.dot(act_all, down_both, preferred_element_type=jnp.float32)
    returned = ring_reduce(down.astype(jnp.bfloat16), "z").astype(jnp.bfloat16)
    returned = pair_reduce(pair_reduce(returned, "hi").astype(jnp.bfloat16), "xlo")
    return (middle_float + returned.astype(jnp.float32)).astype(jnp.bfloat16)


def solution(mesh):
    pool = ("hi", "core")
    chip_mesh = jax.sharding.Mesh(
        mesh.devices.reshape(
            mesh.shape["pool"] // 2, 2, mesh.shape["grp"], mesh.shape["tp"] // 2, 2
        ),
        ("hi", "core", "grp", "z", "xlo"),
    )
    return jax.shard_map(
        body,
        mesh=chip_mesh,
        in_specs=(
            P(pool, "grp"),
            P("grp"),
            P("grp", TP),
            P("grp", TP),
            P("grp", TP),
            P(TP, "grp"),
            P(pool, "grp", TP),
            P(pool, "grp", TP),
            P(pool, "grp", TP),
            P(pool, "grp", TP),
            P(pool),
            P(pool),
            P("grp"),
            P("grp", pool + TP),
            P("grp", pool + TP),
            P(pool + TP, "grp"),
        ),
        out_specs=P(pool + TP, "grp"),
        check_vma=False,
    )
```

profile of v0, /device:TPU:0, one launch (start us, length us, event | category | flops | bytes accessed | tf_op | source)
XLA Modules:
  0.0 316.4 jit_solution(8454081397097080991)
XLA Ops:
  20.3 11.4 %collective-permute-done.5 = f32[64,1280]{1,0:T(8,128)S(1)} collective-permute-done((f32[64,1280]{1,0:T(8,128)S(1)}, f32[64,1280]{1,0:T(8,128)S(1)}, u32[]{:S(2)}, u32[]{:S(2)}) %collective-permute-start.5) | collective-permute-done | bytes 327712 | tf_op jit(solution)/shard_map/ppermute | solution.py:76
  38.8 3.8 %collective-permute-done.8 = bf16[64,1280]{1,0:T(8,128)(2,1)S(1)} collective-permute-done((bf16[64,1280]{1,0:T(8,128)(2,1)S(1)}, bf16[64,1280]{1,0:T(8,128)(2,1)S(1)}, u32[]{:S(2)}, u32[]{:S(2)}) %collective-permute-start.8) | collective-permute-done | bytes 163872 | tf_op jit(solution)/shard_map/ppermute | solution.py:62
  49.5 13.1 %bitcast_reduce_fusion = (f32[2,128,8]{1,2,0:T(8,128)S(1)}, f32[2,128,8,4096]{3,1,2,0:T(8,128)}) fusion(bf16[2,4096,128]{2,1,0:T(8,128)(2,1)S(1)} %copy-done, bf16[2,128,8,128]{3,2,1,0:T(8,128)(2,1)S(1)} %bitcast.249), kind=kOutput, calls=%fused_computation.13 | convolution fusion | flops 2164258816 | bytes 36184064 | tf_op jit(solution)/shard_map/pskgd,pjkd->pskgj/dot_general | solution.py:144
  63.4 4.5 %fusion.94 = (f32[256,8]{1,0:T(8,128)S(1)}, f32[256,8,64]{2,1,0:T(8,128)S(1)}) fusion(bf16[256,8,128]{2,1,0:T(8,128)(2,1)S(1)} %bitcast.248, bf16[256,64,128]{2,1,0:T(8,128)(2,1)} %param.26, pred[256,64]{1,0:T(8,128)(4,1)S(1)} %broadcast_compare_fusion), kind=kOutput, calls=%fused_computation.196 | convolution fusion | flops 33945600 | bytes 5267456 | tf_op jit(solution)/shard_map/skgd,sjkd->skgj/dot_general | solution.py:151
  79.6 15.1 %fusion.24 = f32[2,128,1,8,256]{4,1,3,0,2:T(8,128)} fusion(f32[2,128,8,4096]{3,1,2,0:T(8,128)} %get-tuple-element.42, f32[2,128,8]{1,2,0:T(8,128)S(1)} %copy.102, bf16[2,4096,1,128]{3,1,0,2:T(8,128)(2,1)} %bitcast.301, bf16[256]{0:T(256)(128)(2,1)S(1)} %pad.56.clone), kind=kOutput, calls=%fused_computation.54 | convolution fusion | flops 4328521728 | bytes 37757440 | tf_op jit(solution)/shard_map/pskgj,pjkd->pskgd/dot_general | solution.py:171
  94.7 4.2 %copy.103 = f32[2,128,1,8,256]{4,3,1,0,2:T(8,128)} copy(f32[2,128,1,8,256]{4,1,3,0,2:T(8,128)} %fusion.24) | data formatting | bytes 4194304 | tf_op jit(solution)/shard_map/pskgj,pjkd->pskgd/transpose | solution.py:171
  114.2 6.9 %collective-permute-done.14 = f32[64,1032]{1,0:T(8,128)S(1)} collective-permute-done((f32[64,1032]{1,0:T(8,128)S(1)}, f32[64,1032]{1,0:T(8,128)S(1)}, u32[]{:S(2)}, u32[]{:S(2)}) %collective-permute-start.14) | collective-permute-done | bytes 264224 | tf_op jit(solution)/shard_map/ppermute | solution.py:76
  123.6 3.8 %collective-permute-done.12 = f32[64,1032]{1,0:T(8,128)S(1)} collective-permute-done((f32[64,1032]{1,0:T(8,128)S(1)}, f32[64,1032]{1,0:T(8,128)S(1)}, u32[]{:S(2)}, u32[]{:S(2)}) %collective-permute-start.12) | collective-permute-done | bytes 264224 | tf_op jit(solution)/shard_map/ppermute | solution.py:76
  141.9 4.1 %collective-permute-start.20 = (bf16[64,2048]{1,0:T(8,128)(2,1)S(1)}, bf16[64,2048]{1,0:T(8,128)(2,1)S(1)}, u32[]{:S(2)}, u32[]{:S(2)}) collective-permute-start(bf16[64,2048]{1,0:T(8,128)(2,1)S(1)} %get-tuple-element.34), channel_id=1, source_target_pairs={{0,6},{2,0},{4,2},{6,4},{1,7},{3,1},{5,3},{7,5},{8,14},{10,8},{12,... | collective-permute-start | bytes 786440 | tf_op jit(solution)/shard_map/ppermute | solution.py:76
  147.3 9.6 %collective-permute-done.20 = bf16[64,2048]{1,0:T(8,128)(2,1)S(1)} collective-permute-done((bf16[64,2048]{1,0:T(8,128)(2,1)S(1)}, bf16[64,2048]{1,0:T(8,128)(2,1)S(1)}, u32[]{:S(2)}, u32[]{:S(2)}) %collective-permute-start.20) | collective-permute-done | bytes 262176 | tf_op jit(solution)/shard_map/ppermute | solution.py:76
  184.2 4.4 %collective-permute-done.26 = bf16[64,2048]{1,0:T(8,128)(2,1)S(1)} collective-permute-done((bf16[64,2048]{1,0:T(8,128)(2,1)S(1)}, bf16[64,2048]{1,0:T(8,128)(2,1)S(1)}, u32[]{:S(2)}, u32[]{:S(2)}) %collective-permute-start.26) | collective-permute-done | bytes 262176 | tf_op jit(solution)/shard_map/ppermute | solution.py:39
  193.8 3.8 %copy.113 = bf16[2048,448]{1,0:T(8,128)(2,1)} copy(bf16[2048,448]{0,1:T(8,128)(2,1)} %param.32) | data formatting | bytes 3670016 | tf_op args[14]
  197.9 3.9 %copy.112 = bf16[2048,448]{1,0:T(8,128)(2,1)} copy(bf16[2048,448]{0,1:T(8,128)(2,1)} %collective-permute-done.30) | data formatting | bytes 3670016 | tf_op jit(solution)/shard_map/ppermute | solution.py:211
  201.8 3.8 %copy.114 = bf16[2048,448]{1,0:T(8,128)(2,1)} copy(bf16[2048,448]{0,1:T(8,128)(2,1)} %collective-permute-done.31) | data formatting | bytes 3670016 | tf_op jit(solution)/shard_map/ppermute | solution.py:212
  206.9 5.6 %collective-permute-done.27 = bf16[128,2048]{1,0:T(8,128)(2,1)} collective-permute-done((bf16[128,2048]{1,0:T(8,128)(2,1)S(1)}, bf16[128,2048]{1,0:T(8,128)(2,1)}, u32[]{:S(2)}, u32[]{:S(2)}) %collective-permute-start.27) | collective-permute-done | bytes 524320 | tf_op jit(solution)/shard_map/ppermute | solution.py:62
  216.1 5.4 %fusion.28 = bf16[4,128,896]{2,1,0:T(8,128)(2,1)S(1)} fusion(bf16[4,128,2048]{2,1,0:T(8,128)(2,1)} %gather_fusion.9, bf16[2048,448]{1,0:T(8,128)(2,1)} %copy.112, bf16[2048,448]{1,0:T(8,128)(2,1)} %copy.111), kind=kOutput, calls=%fused_computation.56 | convolution fusion | flops 1886846976 | bytes 6684672 | tf_op jit(solution)/shard_map/dot_general | solution.py:217
  226.5 11.0 %collective-permute-done.34 = bf16[128,1792]{1,0:T(8,128)(2,1)S(1)} collective-permute-done((bf16[128,1792]{1,0:T(8,128)(2,1)S(1)}, bf16[128,1792]{1,0:T(8,128)(2,1)S(1)}, u32[]{:S(2)}, u32[]{:S(2)}) %collective-permute-start.34) | collective-permute-done | bytes 458784 | tf_op jit(solution)/shard_map/ppermute | solution.py:76
  240.3 8.3 %collective-permute-done.32 = bf16[128,1792]{1,0:T(8,128)(2,1)S(1)} collective-permute-done((bf16[128,1792]{1,0:T(8,128)(2,1)S(1)}, bf16[128,1792]{1,0:T(8,128)(2,1)S(1)}, u32[]{:S(2)}, u32[]{:S(2)}) %collective-permute-start.32) | collective-permute-done | bytes 458784 | tf_op jit(solution)/shard_map/ppermute | solution.py:76
  252.2 5.5 %collective-permute-done.37 = bf16[128,896]{1,0:T(8,128)(2,1)S(1)} collective-permute-done((bf16[128,896]{1,0:T(8,128)(2,1)S(1)}, bf16[128,896]{1,0:T(8,128)(2,1)S(1)}, u32[]{:S(2)}, u32[]{:S(2)}) %collective-permute-start.37) | collective-permute-done | bytes 229408 | tf_op jit(solution)/shard_map/ppermute | solution.py:62
  265.0 4.7 %fusion.18 = bf16[512,2048]{1,0:T(8,128)(2,1)S(1)} fusion(bf16[512,896]{1,0:T(8,128)(2,1)} %bitcast.266, bf16[448,2048]{1,0:T(8,128)(2,1)} %collective-permute-done.38, bf16[448,2048]{1,0:T(8,128)(2,1)} %param.33), kind=kOutput, calls=%fused_computation.34 | convolution fusion | flops 1887436800 | bytes 6684672 | tf_op jit(solution)/shard_map/dot_general | solution.py:225
  274.0 13.1 %collective-permute-done.41 = bf16[128,2048]{1,0:T(8,128)(2,1)} collective-permute-done((bf16[128,2048]{1,0:T(8,128)(2,1)}, bf16[128,2048]{1,0:T(8,128)(2,1)}, u32[]{:S(2)}, u32[]{:S(2)}) %collective-permute-start.41) | collective-permute-done | bytes 524320 | tf_op jit(solution)/shard_map/ppermute | solution.py:76
  288.4 10.2 %collective-permute-done.39 = bf16[128,2048]{1,0:T(8,128)(2,1)} collective-permute-done((bf16[128,2048]{1,0:T(8,128)(2,1)S(1)}, bf16[128,2048]{1,0:T(8,128)(2,1)}, u32[]{:S(2)}, u32[]{:S(2)}) %collective-permute-start.39) | collective-permute-done | bytes 524320 | tf_op jit(solution)/shard_map/ppermute | solution.py:76
  300.6 9.7 %collective-permute-done.42 = bf16[64,2048]{1,0:T(8,128)(2,1)S(1)} collective-permute-done((bf16[64,2048]{1,0:T(8,128)(2,1)S(1)}, bf16[64,2048]{1,0:T(8,128)(2,1)S(1)}, u32[]{:S(2)}, u32[]{:S(2)}) %collective-permute-start.42) | collective-permute-done | bytes 262176 | tf_op jit(solution)/shard_map/ppermute | solution.py:52
  310.7 4.8 %collective-permute-done.43 = bf16[32,2048]{1,0:T(8,128)(2,1)S(1)} collective-permute-done((bf16[32,2048]{1,0:T(8,128)(2,1)S(1)}, bf16[32,2048]{1,0:T(8,128)(2,1)S(1)}, u32[]{:S(2)}, u32[]{:S(2)}) %collective-permute-start.43) | collective-permute-done | bytes 131104 | tf_op jit(solution)/shard_map/ppermute | solution.py:52
  (208 shorter events, 145.0 us)
Async XLA Ops:
  16.2 15.5 %collective-permute-start.5 = (f32[64,1280]{1,0:T(8,128)S(1)}, f32[64,1280]{1,0:T(8,128)S(1)}, u32[]{:S(2)}, u32[]{:S(2)}) collective-permute-start(f32[64,1280]{1,0:T(8,128)S(1)} %get-tuple-element.28), channel_id=1, source_target_pairs={{0,24},{8,0},{16,8},{24,16},{1,25},{9,1},{17,9},{25,17},{2,26},{10... | collective-permute-start | bytes 983048 | tf_op jit(solution)/shard_map/ppermute | solution.py:76
  18.5 13.2 %collective-permute-start.4 = (f32[64,1280]{1,0:T(8,128)S(1)}, f32[64,1280]{1,0:T(8,128)S(1)}, u32[]{:S(2)}, u32[]{:S(2)}) collective-permute-start(f32[64,1280]{1,0:T(8,128)S(1)} %get-tuple-element.29), channel_id=1, source_target_pairs={{0,16},{8,24},{16,0},{24,8},{1,17},{9,25},{17,1},{25,9},{2,18},{10... | collective-permute-start | bytes 983048 | tf_op jit(solution)/shard_map/ppermute | solution.py:76
  20.2 15.2 %collective-permute-start.3 = (f32[64,1280]{1,0:T(8,128)S(1)}, f32[64,1280]{1,0:T(8,128)S(1)}, u32[]{:S(2)}, u32[]{:S(2)}) collective-permute-start(f32[64,1280]{1,0:T(8,128)S(1)} %get-tuple-element.27), channel_id=1, source_target_pairs={{0,8},{8,16},{16,24},{24,0},{1,9},{9,17},{17,25},{25,1},{2,10},{10... | collective-permute-start | bytes 983048 | tf_op jit(solution)/shard_map/ppermute | solution.py:76
  111.1 9.9 %collective-permute-start.14 = (f32[64,1032]{1,0:T(8,128)S(1)}, f32[64,1032]{1,0:T(8,128)S(1)}, u32[]{:S(2)}, u32[]{:S(2)}) collective-permute-start(f32[64,1032]{1,0:T(8,128)S(1)} %get-tuple-element.32), channel_id=1, source_target_pairs={{0,24},{8,0},{16,8},{24,16},{1,25},{9,1},{17,9},{25,17},{2,26},{10... | collective-permute-start | bytes 792584 | tf_op jit(solution)/shard_map/ppermute | solution.py:76
  112.1 11.4 %collective-permute-start.13 = (f32[64,1032]{1,0:T(8,128)S(1)}, f32[64,1032]{1,0:T(8,128)S(1)}, u32[]{:S(2)}, u32[]{:S(2)}) collective-permute-start(f32[64,1032]{1,0:T(8,128)S(1)} %get-tuple-element.31), channel_id=1, source_target_pairs={{0,16},{8,24},{16,0},{24,8},{1,17},{9,25},{17,1},{25,9},{2,18},{10... | collective-permute-start | bytes 792584 | tf_op jit(solution)/shard_map/ppermute | solution.py:76
  113.3 14.1 %collective-permute-start.12 = (f32[64,1032]{1,0:T(8,128)S(1)}, f32[64,1032]{1,0:T(8,128)S(1)}, u32[]{:S(2)}, u32[]{:S(2)}) collective-permute-start(f32[64,1032]{1,0:T(8,128)S(1)} %get-tuple-element.30), channel_id=1, source_target_pairs={{0,8},{8,16},{16,24},{24,0},{1,9},{9,17},{17,25},{25,1},{2,10},{10... | collective-permute-start | bytes 792584 | tf_op jit(solution)/shard_map/ppermute | solution.py:76
  141.9 15.0 %collective-permute-start.20 = (bf16[64,2048]{1,0:T(8,128)(2,1)S(1)}, bf16[64,2048]{1,0:T(8,128)(2,1)S(1)}, u32[]{:S(2)}, u32[]{:S(2)}) collective-permute-start(bf16[64,2048]{1,0:T(8,128)(2,1)S(1)} %get-tuple-element.34), channel_id=1, source_target_pairs={{0,6},{2,0},{4,2},{6,4},{1,7},{3,1},{5,3},{7,5},{8,14},{10,8},{12,... | collective-permute-start | bytes 786440 | tf_op jit(solution)/shard_map/ppermute | solution.py:76
  146.1 10.9 %collective-permute-start.19 = (bf16[64,2048]{1,0:T(8,128)(2,1)S(1)}, bf16[64,2048]{1,0:T(8,128)(2,1)S(1)}, u32[]{:S(2)}, u32[]{:S(2)}) collective-permute-start(bf16[64,2048]{1,0:T(8,128)(2,1)S(1)} %get-tuple-element.35), channel_id=1, source_target_pairs={{0,4},{2,6},{4,0},{6,2},{1,5},{3,7},{5,1},{7,3},{8,12},{10,14},{12... | collective-permute-start | bytes 786440 | tf_op jit(solution)/shard_map/ppermute | solution.py:76
  146.1 14.4 %collective-permute-start.18 = (bf16[64,2048]{1,0:T(8,128)(2,1)S(1)}, bf16[64,2048]{1,0:T(8,128)(2,1)}, u32[]{:S(2)}, u32[]{:S(2)}) collective-permute-start(bf16[64,2048]{1,0:T(8,128)(2,1)S(1)} %get-tuple-element.33), channel_id=1, source_target_pairs={{0,2},{2,4},{4,6},{6,0},{1,3},{3,5},{5,7},{7,1},{8,10},{10,12},{12... | collective-permute-start | bytes 786440 | tf_op jit(solution)/shard_map/ppermute | solution.py:76
  163.3 34.5 %collective-permute-start.30 = (bf16[2048,448]{0,1:T(8,128)(2,1)}, bf16[2048,448]{0,1:T(8,128)(2,1)}, u32[]{:S(2)}, u32[]{:S(2)}) collective-permute-start(bf16[2048,448]{0,1:T(8,128)(2,1)} %param.31), channel_id=1, source_target_pairs={{0,32},{32,0},{1,33},{33,1},{2,34},{34,2},{3,35},{35,3},{4,36},{36... | collective-permute-start | bytes 5505032 | tf_op jit(solution)/shard_map/ppermute | solution.py:211
  163.3 38.4 %collective-permute-start.31 = (bf16[2048,448]{0,1:T(8,128)(2,1)}, bf16[2048,448]{0,1:T(8,128)(2,1)}, u32[]{:S(2)}, u32[]{:S(2)}) collective-permute-start(bf16[2048,448]{0,1:T(8,128)(2,1)} %param.32), channel_id=1, source_target_pairs={{0,32},{32,0},{1,33},{33,1},{2,34},{34,2},{3,35},{35,3},{4,36},{36... | collective-permute-start | bytes 5505032 | tf_op jit(solution)/shard_map/ppermute | solution.py:212
  188.8 16.8 %collective-permute-start.29 = (bf16[128,2048]{1,0:T(8,128)(2,1)S(1)}, bf16[128,2048]{1,0:T(8,128)(2,1)}, u32[]{:S(2)}, u32[]{:S(2)}) collective-permute-start(bf16[128,2048]{1,0:T(8,128)(2,1)S(1)} %maximum_select_fusion.1), channel_id=1, source_target_pairs={{0,6},{2,0},{4,2},{6,4},{1,7},{3,1},{5,3},{7,5},{8,14},{10,8},{12,... | collective-permute-start | bytes 1572872 | tf_op jit(solution)/shard_map/ppermute | solution.py:62
  190.5 16.4 %collective-permute-start.28 = (bf16[128,2048]{1,0:T(8,128)(2,1)S(1)}, bf16[128,2048]{1,0:T(8,128)(2,1)}, u32[]{:S(2)}, u32[]{:S(2)}) collective-permute-start(bf16[128,2048]{1,0:T(8,128)(2,1)S(1)} %maximum_select_fusion.1), channel_id=1, source_target_pairs={{0,4},{2,6},{4,0},{6,2},{1,5},{3,7},{5,1},{7,3},{8,12},{10,14},{12... | collective-permute-start | bytes 1572872 | tf_op jit(solution)/shard_map/ppermute | solution.py:62
  190.7 21.7 %collective-permute-start.27 = (bf16[128,2048]{1,0:T(8,128)(2,1)S(1)}, bf16[128,2048]{1,0:T(8,128)(2,1)}, u32[]{:S(2)}, u32[]{:S(2)}) collective-permute-start(bf16[128,2048]{1,0:T(8,128)(2,1)S(1)} %maximum_select_fusion.1), channel_id=1, source_target_pairs={{0,2},{2,4},{4,6},{6,0},{1,3},{3,5},{5,7},{7,1},{8,10},{10,12},{12... | collective-permute-start | bytes 1572872 | tf_op jit(solution)/shard_map/ppermute | solution.py:62
  197.8 67.2 %collective-permute-start.38 = (bf16[448,2048]{1,0:T(8,128)(2,1)}, bf16[448,2048]{1,0:T(8,128)(2,1)}, u32[]{:S(2)}, u32[]{:S(2)}) collective-permute-start(bf16[448,2048]{1,0:T(8,128)(2,1)} %param.33), channel_id=1, source_target_pairs={{0,32},{32,0},{1,33},{33,1},{2,34},{34,2},{3,35},{35,3},{4,36},{36... | collective-permute-start | bytes 5505032 | tf_op jit(solution)/shard_map/ppermute | solution.py:213
  224.1 13.5 %collective-permute-start.34 = (bf16[128,1792]{1,0:T(8,128)(2,1)S(1)}, bf16[128,1792]{1,0:T(8,128)(2,1)S(1)}, u32[]{:S(2)}, u32[]{:S(2)}) collective-permute-start(bf16[128,1792]{1,0:T(8,128)(2,1)S(1)} %get-tuple-element.26), channel_id=1, source_target_pairs={{0,24},{8,0},{16,8},{24,16},{1,25},{9,1},{17,9},{25,17},{2,26},{10... | collective-permute-start | bytes 1376264 | tf_op jit(solution)/shard_map/ppermute | solution.py:76
  225.3 14.9 %collective-permute-start.33 = (bf16[128,1792]{1,0:T(8,128)(2,1)S(1)}, bf16[128,1792]{1,0:T(8,128)(2,1)S(1)}, u32[]{:S(2)}, u32[]{:S(2)}) collective-permute-start(bf16[128,1792]{1,0:T(8,128)(2,1)S(1)} %get-tuple-element.25), channel_id=1, source_target_pairs={{0,16},{8,24},{16,0},{24,8},{1,17},{9,25},{17,1},{25,9},{2,18},{10... | collective-permute-start | bytes 1376264 | tf_op jit(solution)/shard_map/ppermute | solution.py:76
  226.5 22.0 %collective-permute-start.32 = (bf16[128,1792]{1,0:T(8,128)(2,1)S(1)}, bf16[128,1792]{1,0:T(8,128)(2,1)S(1)}, u32[]{:S(2)}, u32[]{:S(2)}) collective-permute-start(bf16[128,1792]{1,0:T(8,128)(2,1)S(1)} %get-tuple-element.24), channel_id=1, source_target_pairs={{0,8},{8,16},{16,24},{24,0},{1,9},{9,17},{17,25},{25,1},{2,10},{10... | collective-permute-start | bytes 1376264 | tf_op jit(solution)/shard_map/ppermute | solution.py:76
  249.8 10.0 %collective-permute-start.36 = (bf16[128,896]{1,0:T(8,128)(2,1)S(1)}, bf16[128,896]{1,0:T(8,128)(2,1)S(1)}, u32[]{:S(2)}, u32[]{:S(2)}) collective-permute-start(bf16[128,896]{1,0:T(8,128)(2,1)S(1)} %fusion.48), channel_id=1, source_target_pairs={{0,16},{8,24},{16,0},{24,8},{1,17},{9,25},{17,1},{25,9},{2,18},{10... | collective-permute-start | bytes 688136 | tf_op jit(solution)/shard_map/ppermute | solution.py:62
  251.3 12.0 %collective-permute-start.35 = (bf16[128,896]{1,0:T(8,128)(2,1)S(1)}, bf16[128,896]{1,0:T(8,128)(2,1)S(1)}, u32[]{:S(2)}, u32[]{:S(2)}) collective-permute-start(bf16[128,896]{1,0:T(8,128)(2,1)S(1)} %fusion.48), channel_id=1, source_target_pairs={{0,8},{8,16},{16,24},{24,0},{1,9},{9,17},{17,25},{25,1},{2,10},{10... | collective-permute-start | bytes 688136 | tf_op jit(solution)/shard_map/ppermute | solution.py:62
  271.9 15.1 %collective-permute-start.41 = (bf16[128,2048]{1,0:T(8,128)(2,1)}, bf16[128,2048]{1,0:T(8,128)(2,1)}, u32[]{:S(2)}, u32[]{:S(2)}) collective-permute-start(bf16[128,2048]{1,0:T(8,128)(2,1)} %get-tuple-element.22), channel_id=1, source_target_pairs={{0,6},{2,0},{4,2},{6,4},{1,7},{3,1},{5,3},{7,5},{8,14},{10,8},{12,... | collective-permute-start | bytes 1572872 | tf_op jit(solution)/shard_map/ppermute | solution.py:76
  271.9 16.4 %collective-permute-start.40 = (bf16[128,2048]{1,0:T(8,128)(2,1)S(1)}, bf16[128,2048]{1,0:T(8,128)(2,1)}, u32[]{:S(2)}, u32[]{:S(2)}) collective-permute-start(bf16[128,2048]{1,0:T(8,128)(2,1)S(1)} %get-tuple-element.23), channel_id=1, source_target_pairs={{0,4},{2,6},{4,0},{6,2},{1,5},{3,7},{5,1},{7,3},{8,12},{10,14},{12... | collective-permute-start | bytes 1572872 | tf_op jit(solution)/shard_map/ppermute | solution.py:76
  272.6 26.1 %collective-permute-start.39 = (bf16[128,2048]{1,0:T(8,128)(2,1)S(1)}, bf16[128,2048]{1,0:T(8,128)(2,1)}, u32[]{:S(2)}, u32[]{:S(2)}) collective-permute-start(bf16[128,2048]{1,0:T(8,128)(2,1)S(1)} %get-tuple-element.21), channel_id=1, source_target_pairs={{0,2},{2,4},{4,6},{6,0},{1,3},{3,5},{5,7},{7,1},{8,10},{10,12},{12... | collective-permute-start | bytes 1572872 | tf_op jit(solution)/shard_map/ppermute | solution.py:76
  300.5 9.8 %collective-permute-start.42 = (bf16[64,2048]{1,0:T(8,128)(2,1)S(1)}, bf16[64,2048]{1,0:T(8,128)(2,1)S(1)}, u32[]{:S(2)}, u32[]{:S(2)}) collective-permute-start(bf16[64,2048]{1,0:T(8,128)(2,1)S(1)} %dynamic-slice_bitcast_fusion.6), channel_id=1, source_target_pairs={{0,64},{64,0},{1,65},{65,1},{2,66},{66,2},{3,67},{67,3},{4,68},{68... | collective-permute-start | bytes 786440 | tf_op jit(solution)/shard_map/ppermute | solution.py:52
  (37 other events, 355.1 us)
where the time goes:
time: 322 us; the launch traced here: 316 us
  waiting for transfers between devices  154 us (48%)
  matrix products  56.4 us (18%)
  starting transfers between devices  48.8 us (15%)
  local copies, waits for them, and re-layouts  40.6 us (13%)
  other arithmetic  15.4 us (5%)
    ppermute x15, waiting for transfers between devices, ring_reduce(): total = total + lax.ppermute(outgoing, axis, pairs).astype(jnp.float32)  88.1 us
    ppermute x21, waiting for transfers between devices, ring_gather(): pieces.append(lax.ppermute(part, axis, pairs))  42.2 us
    ppermute x21, starting transfers between devices, ring_gather(): pieces.append(lax.ppermute(part, axis, pairs))  24.1 us
    ppermute x15, starting transfers between devices, ring_reduce(): total = total + lax.ppermute(outgoing, axis, pairs).astype(jnp.float32)  17 us
    ppermute x3, waiting for transfers between devices, pair_reduce(): other = lax.ppermute(other.astype(jnp.bfloat16), axis, swap)  16 us
    dot_general x1, matrix products, body(): jnp.einsum('pskgj,pjkd->pskgd', pre_weights, pre_value_ext, preferred_ele...  15.1 us
    dot_general x1, matrix products, body(): jnp.einsum('pskgd,pjkd->pskgj', grouped, pre_key, preferred_element_type=...  13.1 us
    unnamed x38, local copies, waits for them, and re-layouts  8.02 us
  transfers between devices with their start and end apart: 44, of which 35 were waited for; matrix products, arithmetic and copies ran while one was open for 11% of the time, Pallas kernels for 0%

commit v1 on v0

--- a/solution.py
+++ b/solution.py
@@ -208,21 +208,25 @@
     ffn_inverse = lax.rsqrt(ffn_squares / D + epsilon)
     normed_own = (middle_float * ffn_inverse[:, None] * ffn_gain).astype(jnp.bfloat16)
     swap = [(0, 1), (1, 0)]
-    gate_both = jnp.concatenate([w_gate, lax.ppermute(w_gate, "core", swap)], axis=1)
-    up_both = jnp.concatenate([w_up, lax.ppermute(w_up, "core", swap)], axis=1)
-    down_both = jnp.concatenate([w_down, lax.ppermute(w_down, "core", swap)], axis=0)
+    other_gate = lax.ppermute(w_gate, "core", swap)
+    other_up = lax.ppermute(w_up, "core", swap)
+    other_down = lax.ppermute(w_down, "core", swap)
     normed_row = pair_gather(pair_gather(normed_own, "xlo"), "hi")
     normed_half = ring_gather(normed_row, "z")
-    hidden_units = gate_both.shape[1]
-    part_gate = jnp.dot(normed_half, gate_both, preferred_element_type=jnp.float32)
-    part_upward = jnp.dot(normed_half, up_both, preferred_element_type=jnp.float32)
-    both = jnp.concatenate([part_gate, part_upward], axis=1).astype(jnp.bfloat16)
+    hidden_units = 2 * w_gate.shape[1]
+    pieces = [
+        jnp.dot(normed_half, weight, preferred_element_type=jnp.float32)
+        for weight in (w_gate, other_gate, w_up, other_up)
+    ]
+    both = jnp.concatenate(pieces, axis=1).astype(jnp.bfloat16)
     reduced = ring_reduce(both, "grp")
     gate = reduced[:, :hidden_units]
     upward = reduced[:, hidden_units:]
     act = (jax.nn.silu(gate) * upward).astype(jnp.bfloat16)
     act_all = ring_gather(act, "grp")
-    down = jnp.dot(act_all, down_both, preferred_element_type=jnp.float32)
+    own_units = w_down.shape[0]
+    down = jnp.dot(act_all[:, :own_units], w_down, preferred_element_type=jnp.float32)
+    down = down + jnp.dot(act_all[:, own_units:], other_down, preferred_element_type=jnp.float32)
     returned = ring_reduce(down.astype(jnp.bfloat16), "z").astype(jnp.bfloat16)
     returned = pair_reduce(pair_reduce(returned, "hi").astype(jnp.bfloat16), "xlo")
     return (middle_float + returned.astype(jnp.float32)).astype(jnp.bfloat16)

time: 322 us -> 324 us (level)
  waiting for transfers between devices: 154 us -> 169 us
  local copies, waits for them, and re-layouts: 40.6 us -> 26.7 us
    ppermute x21, waiting for transfers between devices: 42.2 us -> 56.3 us  [ring_gather(): pieces.append(lax.ppermute(part, axis, pairs))]
    ppermute x2 -> x0, local copies, waits for them, and re-layouts: 7.69 us -> none  [the longest x1 3.87 us: body(): lax.ppermute(w_gate, 'core', swap)]
    unnamed x38 -> x32, local copies, waits for them, and re-layouts: 8.02 us -> 1.81 us
    dot_general x3 -> x6, matrix products: 12.5 us -> 15.5 us  [the longest x4 9.87 us: body(): jnp.dot(normed_half, weight, preferred_element_type=jnp.float32)]
    gather x7 -> x8, local copies, waits for them, and re-layouts: 6.5 us -> 6.22 us  [ring_gather(): return stacked[order].reshape((size * part.shape[0],) + part.shape[1:])]
  transfers between devices with their start and end apart: 44 -> 44, of which waited for: 35 -> 36; matrix products, arithmetic and copies ran while one was open for 11% -> 7% of each run, Pallas kernels for 0% -> 0%
where the time goes in v1:
time: 324 us; the launch traced here: 319 us
  waiting for transfers between devices  169 us (52%)
  matrix products  59.4 us (18%)
  starting transfers between devices  48.2 us (15%)
  local copies, waits for them, and re-layouts  26.7 us (8%)
  other arithmetic  14.1 us (4%)
    ppermute x15, waiting for transfers between devices, ring_reduce(): total = total + lax.ppermute(outgoing, axis, pairs).astype(jnp.float32)  88 us
    ppermute x21, waiting for transfers between devices, ring_gather(): pieces.append(lax.ppermute(part, axis, pairs))  56.3 us
    ppermute x21, starting transfers between devices, ring_gather(): pieces.append(lax.ppermute(part, axis, pairs))  23.7 us
    ppermute x15, starting transfers between devices, ring_reduce(): total = total + lax.ppermute(outgoing, axis, pairs).astype(jnp.float32)  17.5 us
    ppermute x3, waiting for transfers between devices, pair_reduce(): other = lax.ppermute(other.astype(jnp.bfloat16), axis, swap)  16.7 us
    dot_general x1, matrix products, body(): jnp.einsum('pskgj,pjkd->pskgd', pre_weights, pre_value_ext, preferred_ele...  15.1 us
    dot_general x1, matrix products, body(): jnp.einsum('pskgd,pjkd->pskgj', grouped, pre_key, preferred_element_type=...  13.1 us
    dot_general x4, matrix products, body(): jnp.dot(normed_half, weight, preferred_element_type=jnp.float32)  9.87 us
  transfers between devices with their start and end apart: 44, of which 36 were waited for; matrix products, arithmetic and copies ran while one was open for 7% of the time, Pallas kernels for 0%

profile of v1, /device:TPU:0, one launch (start us, length us, event | category | flops | bytes accessed | tf_op | source)
XLA Modules:
  0.0 318.6 jit_solution(12000697373245590163)
XLA Ops:
  20.3 11.4 %collective-permute-done.5 = f32[64,1280]{1,0:T(8,128)S(1)} collective-permute-done((f32[64,1280]{1,0:T(8,128)S(1)}, f32[64,1280]{1,0:T(8,128)S(1)}, u32[]{:S(2)}, u32[]{:S(2)}) %collective-permute-start.5) | collective-permute-done | bytes 327712 | tf_op jit(solution)/shard_map/ppermute | solution.py:76
  31.7 3.7 %collective-permute-done.3 = f32[64,1280]{1,0:T(8,128)S(1)} collective-permute-done((f32[64,1280]{1,0:T(8,128)S(1)}, f32[64,1280]{1,0:T(8,128)S(1)}, u32[]{:S(2)}, u32[]{:S(2)}) %collective-permute-start.3) | collective-permute-done | bytes 327712 | tf_op jit(solution)/shard_map/ppermute | solution.py:76
  38.8 3.8 %collective-permute-done.8 = bf16[64,1280]{1,0:T(8,128)(2,1)S(1)} collective-permute-done((bf16[64,1280]{1,0:T(8,128)(2,1)S(1)}, bf16[64,1280]{1,0:T(8,128)(2,1)S(1)}, u32[]{:S(2)}, u32[]{:S(2)}) %collective-permute-start.8) | collective-permute-done | bytes 163872 | tf_op jit(solution)/shard_map/ppermute | solution.py:62
  49.5 13.1 %bitcast_reduce_fusion = (f32[2,128,8]{1,2,0:T(8,128)S(1)}, f32[2,128,8,4096]{3,1,2,0:T(8,128)}) fusion(bf16[2,4096,128]{2,1,0:T(8,128)(2,1)S(1)} %copy-done, bf16[2,128,8,128]{3,2,1,0:T(8,128)(2,1)S(1)} %bitcast.264), kind=kOutput, calls=%fused_computation.13 | convolution fusion | flops 2164258816 | bytes 36184064 | tf_op jit(solution)/shard_map/pskgd,pjkd->pskgj/dot_general | solution.py:144
  63.5 4.5 %fusion.91 = (f32[256,8]{1,0:T(8,128)S(1)}, f32[256,8,64]{2,1,0:T(8,128)S(1)}) fusion(bf16[256,8,128]{2,1,0:T(8,128)(2,1)S(1)} %bitcast.261, bf16[256,64,128]{2,1,0:T(8,128)(2,1)} %param.26, pred[256,64]{1,0:T(8,128)(4,1)S(1)} %broadcast_compare_fusion), kind=kOutput, calls=%fused_computation.182 | convolution fusion | flops 33945600 | bytes 5267456 | tf_op jit(solution)/shard_map/skgd,sjkd->skgj/dot_general | solution.py:151
  79.4 15.1 %fusion.19 = f32[2,128,1,8,256]{4,1,3,0,2:T(8,128)} fusion(f32[2,128,8,4096]{3,1,2,0:T(8,128)} %get-tuple-element.42, f32[2,128,8]{1,2,0:T(8,128)S(1)} %copy.86, bf16[2,4096,1,128]{3,1,0,2:T(8,128)(2,1)} %bitcast.316, bf16[256]{0:T(256)(128)(2,1)S(1)} %pad.52.clone), kind=kOutput, calls=%fused_computation.43 | convolution fusion | flops 4328521728 | bytes 37757440 | tf_op jit(solution)/shard_map/pskgj,pjkd->pskgd/dot_general | solution.py:171
  94.5 4.2 %copy.87 = f32[2,128,1,8,256]{4,3,1,0,2:T(8,128)} copy(f32[2,128,1,8,256]{4,1,3,0,2:T(8,128)} %fusion.19) | data formatting | bytes 4194304 | tf_op jit(solution)/shard_map/pskgj,pjkd->pskgd/transpose | solution.py:171
  98.7 3.7 %gather_fusion.6 = f32[256,8,256]{2,1,0:T(8,128)} fusion(f32[256,8,256]{2,1,0:T(8,128)} %bitcast.254, s32[1024]{0:T(1024)S(1)} %pad_clamp_fusion.1), kind=kCustom, calls=%fused_computation.6 | custom fusion | bytes 4195328 | tf_op jit(solution)/shard_map/gather | solution.py:174
  114.2 6.7 %collective-permute-done.14 = f32[64,1032]{1,0:T(8,128)S(1)} collective-permute-done((f32[64,1032]{1,0:T(8,128)S(1)}, f32[64,1032]{1,0:T(8,128)S(1)}, u32[]{:S(2)}, u32[]{:S(2)}) %collective-permute-start.14) | collective-permute-done | bytes 264224 | tf_op jit(solution)/shard_map/ppermute | solution.py:76
  123.5 3.7 %collective-permute-done.12 = f32[64,1032]{1,0:T(8,128)S(1)} collective-permute-done((f32[64,1032]{1,0:T(8,128)S(1)}, f32[64,1032]{1,0:T(8,128)S(1)}, u32[]{:S(2)}, u32[]{:S(2)}) %collective-permute-start.12) | collective-permute-done | bytes 264224 | tf_op jit(solution)/shard_map/ppermute | solution.py:76
  141.7 4.1 %collective-permute-start.20 = (bf16[64,2048]{1,0:T(8,128)(2,1)S(1)}, bf16[64,2048]{1,0:T(8,128)(2,1)S(1)}, u32[]{:S(2)}, u32[]{:S(2)}) collective-permute-start(bf16[64,2048]{1,0:T(8,128)(2,1)S(1)} %get-tuple-element.34), channel_id=1, source_target_pairs={{0,6},{2,0},{4,2},{6,4},{1,7},{3,1},{5,3},{7,5},{8,14},{10,8},{12,... | collective-permute-start | bytes 786440 | tf_op jit(solution)/shard_map/ppermute | solution.py:76
  147.1 9.5 %collective-permute-done.20 = bf16[64,2048]{1,0:T(8,128)(2,1)S(1)} collective-permute-done((bf16[64,2048]{1,0:T(8,128)(2,1)S(1)}, bf16[64,2048]{1,0:T(8,128)(2,1)S(1)}, u32[]{:S(2)}, u32[]{:S(2)}) %collective-permute-start.20) | collective-permute-done | bytes 262176 | tf_op jit(solution)/shard_map/ppermute | solution.py:76
  156.6 3.5 %collective-permute-done.18 = bf16[64,2048]{1,0:T(8,128)(2,1)} collective-permute-done((bf16[64,2048]{1,0:T(8,128)(2,1)S(1)}, bf16[64,2048]{1,0:T(8,128)(2,1)}, u32[]{:S(2)}, u32[]{:S(2)}) %collective-permute-start.18) | collective-permute-done | bytes 262176 | tf_op jit(solution)/shard_map/ppermute | solution.py:76
  176.6 3.5 %collective-permute-done.25 = bf16[32,2048]{1,0:T(8,128)(2,1)S(1)} collective-permute-done((bf16[32,2048]{1,0:T(8,128)(2,1)S(1)}, bf16[32,2048]{1,0:T(8,128)(2,1)S(1)}, u32[]{:S(2)}, u32[]{:S(2)}) %collective-permute-start.25) | collective-permute-done | bytes 131104 | tf_op jit(solution)/shard_map/ppermute | solution.py:39
  183.6 4.5 %collective-permute-done.26 = bf16[64,2048]{1,0:T(8,128)(2,1)S(1)} collective-permute-done((bf16[64,2048]{1,0:T(8,128)(2,1)S(1)}, bf16[64,2048]{1,0:T(8,128)(2,1)S(1)}, u32[]{:S(2)}, u32[]{:S(2)}) %collective-permute-start.26) | collective-permute-done | bytes 262176 | tf_op jit(solution)/shard_map/ppermute | solution.py:39
  191.1 11.9 %collective-permute-done.29 = bf16[128,2048]{1,0:T(8,128)(2,1)S(1)} collective-permute-done((bf16[128,2048]{1,0:T(8,128)(2,1)S(1)}, bf16[128,2048]{1,0:T(8,128)(2,1)S(1)}, u32[]{:S(2)}, u32[]{:S(2)}) %collective-permute-start.29) | collective-permute-done | bytes 524320 | tf_op jit(solution)/shard_map/ppermute | solution.py:62
  206.3 5.9 %collective-permute-done.27 = bf16[128,2048]{1,0:T(8,128)(2,1)S(1)} collective-permute-done((bf16[128,2048]{1,0:T(8,128)(2,1)S(1)}, bf16[128,2048]{1,0:T(8,128)(2,1)S(1)}, u32[]{:S(2)}, u32[]{:S(2)}) %collective-permute-start.27) | collective-permute-done | bytes 524320 | tf_op jit(solution)/shard_map/ppermute | solution.py:62
  227.5 10.7 %collective-permute-done.34 = bf16[128,1792]{0,1:T(8,128)(2,1)S(1)} collective-permute-done((bf16[128,1792]{0,1:T(8,128)(2,1)S(1)}, bf16[128,1792]{0,1:T(8,128)(2,1)S(1)}, u32[]{:S(2)}, u32[]{:S(2)}) %collective-permute-start.34) | collective-permute-done | bytes 458784 | tf_op jit(solution)/shard_map/ppermute | solution.py:76
  241.3 8.3 %collective-permute-done.32 = bf16[128,1792]{0,1:T(8,128)(2,1)S(1)} collective-permute-done((bf16[128,1792]{0,1:T(8,128)(2,1)S(1)}, bf16[128,1792]{0,1:T(8,128)(2,1)S(1)}, u32[]{:S(2)}, u32[]{:S(2)}) %collective-permute-start.32) | collective-permute-done | bytes 458784 | tf_op jit(solution)/shard_map/ppermute | solution.py:76
  253.2 5.3 %collective-permute-done.37 = bf16[128,896]{0,1:T(8,128)(2,1)S(1)} collective-permute-done((bf16[128,896]{0,1:T(8,128)(2,1)S(1)}, bf16[128,896]{0,1:T(8,128)(2,1)S(1)}, u32[]{:S(2)}, u32[]{:S(2)}) %collective-permute-start.37) | collective-permute-done | bytes 229408 | tf_op jit(solution)/shard_map/ppermute | solution.py:62
  275.7 13.1 %collective-permute-done.41 = bf16[128,2048]{1,0:T(8,128)(2,1)} collective-permute-done((bf16[128,2048]{1,0:T(8,128)(2,1)}, bf16[128,2048]{1,0:T(8,128)(2,1)}, u32[]{:S(2)}, u32[]{:S(2)}) %collective-permute-start.41) | collective-permute-done | bytes 524320 | tf_op jit(solution)/shard_map/ppermute | solution.py:76
  290.3 10.2 %collective-permute-done.39 = bf16[128,2048]{1,0:T(8,128)(2,1)} collective-permute-done((bf16[128,2048]{1,0:T(8,128)(2,1)S(1)}, bf16[128,2048]{1,0:T(8,128)(2,1)}, u32[]{:S(2)}, u32[]{:S(2)}) %collective-permute-start.39) | collective-permute-done | bytes 524320 | tf_op jit(solution)/shard_map/ppermute | solution.py:76
  302.5 9.7 %collective-permute-done.42 = bf16[64,2048]{1,0:T(8,128)(2,1)S(1)} collective-permute-done((bf16[64,2048]{1,0:T(8,128)(2,1)S(1)}, bf16[64,2048]{1,0:T(8,128)(2,1)S(1)}, u32[]{:S(2)}, u32[]{:S(2)}) %collective-permute-start.42) | collective-permute-done | bytes 262176 | tf_op jit(solution)/shard_map/ppermute | solution.py:52
  312.4 5.0 %collective-permute-done.43 = bf16[32,2048]{1,0:T(8,128)(2,1)S(1)} collective-permute-done((bf16[32,2048]{1,0:T(8,128)(2,1)S(1)}, bf16[32,2048]{1,0:T(8,128)(2,1)S(1)}, u32[]{:S(2)}, u32[]{:S(2)}) %collective-permute-start.43) | collective-permute-done | bytes 131104 | tf_op jit(solution)/shard_map/ppermute | solution.py:52
  (205 shorter events, 142.3 us)
Async XLA Ops:
  16.2 15.5 %collective-permute-start.5 = (f32[64,1280]{1,0:T(8,128)S(1)}, f32[64,1280]{1,0:T(8,128)S(1)}, u32[]{:S(2)}, u32[]{:S(2)}) collective-permute-start(f32[64,1280]{1,0:T(8,128)S(1)} %get-tuple-element.28), channel_id=1, source_target_pairs={{0,24},{8,0},{16,8},{24,16},{1,25},{9,1},{17,9},{25,17},{2,26},{10... | collective-permute-start | bytes 983048 | tf_op jit(solution)/shard_map/ppermute | solution.py:76
  18.5 13.2 %collective-permute-start.4 = (f32[64,1280]{1,0:T(8,128)S(1)}, f32[64,1280]{1,0:T(8,128)S(1)}, u32[]{:S(2)}, u32[]{:S(2)}) collective-permute-start(f32[64,1280]{1,0:T(8,128)S(1)} %get-tuple-element.29), channel_id=1, source_target_pairs={{0,16},{8,24},{16,0},{24,8},{1,17},{9,25},{17,1},{25,9},{2,18},{10... | collective-permute-start | bytes 983048 | tf_op jit(solution)/shard_map/ppermute | solution.py:76
  20.2 15.2 %collective-permute-start.3 = (f32[64,1280]{1,0:T(8,128)S(1)}, f32[64,1280]{1,0:T(8,128)S(1)}, u32[]{:S(2)}, u32[]{:S(2)}) collective-permute-start(f32[64,1280]{1,0:T(8,128)S(1)} %get-tuple-element.27), channel_id=1, source_target_pairs={{0,8},{8,16},{16,24},{24,0},{1,9},{9,17},{17,25},{25,1},{2,10},{10... | collective-permute-start | bytes 983048 | tf_op jit(solution)/shard_map/ppermute | solution.py:76
  110.9 10.0 %collective-permute-start.14 = (f32[64,1032]{1,0:T(8,128)S(1)}, f32[64,1032]{1,0:T(8,128)S(1)}, u32[]{:S(2)}, u32[]{:S(2)}) collective-permute-start(f32[64,1032]{1,0:T(8,128)S(1)} %get-tuple-element.32), channel_id=1, source_target_pairs={{0,24},{8,0},{16,8},{24,16},{1,25},{9,1},{17,9},{25,17},{2,26},{10... | collective-permute-start | bytes 792584 | tf_op jit(solution)/shard_map/ppermute | solution.py:76
  112.0 11.4 %collective-permute-start.13 = (f32[64,1032]{1,0:T(8,128)S(1)}, f32[64,1032]{1,0:T(8,128)S(1)}, u32[]{:S(2)}, u32[]{:S(2)}) collective-permute-start(f32[64,1032]{1,0:T(8,128)S(1)} %get-tuple-element.31), channel_id=1, source_target_pairs={{0,16},{8,24},{16,0},{24,8},{1,17},{9,25},{17,1},{25,9},{2,18},{10... | collective-permute-start | bytes 792584 | tf_op jit(solution)/shard_map/ppermute | solution.py:76
  113.3 13.8 %collective-permute-start.12 = (f32[64,1032]{1,0:T(8,128)S(1)}, f32[64,1032]{1,0:T(8,128)S(1)}, u32[]{:S(2)}, u32[]{:S(2)}) collective-permute-start(f32[64,1032]{1,0:T(8,128)S(1)} %get-tuple-element.30), channel_id=1, source_target_pairs={{0,8},{8,16},{16,24},{24,0},{1,9},{9,17},{17,25},{25,1},{2,10},{10... | collective-permute-start | bytes 792584 | tf_op jit(solution)/shard_map/ppermute | solution.py:76
  141.7 14.9 %collective-permute-start.20 = (bf16[64,2048]{1,0:T(8,128)(2,1)S(1)}, bf16[64,2048]{1,0:T(8,128)(2,1)S(1)}, u32[]{:S(2)}, u32[]{:S(2)}) collective-permute-start(bf16[64,2048]{1,0:T(8,128)(2,1)S(1)} %get-tuple-element.34), channel_id=1, source_target_pairs={{0,6},{2,0},{4,2},{6,4},{1,7},{3,1},{5,3},{7,5},{8,14},{10,8},{12,... | collective-permute-start | bytes 786440 | tf_op jit(solution)/shard_map/ppermute | solution.py:76
  145.8 10.8 %collective-permute-start.19 = (bf16[64,2048]{1,0:T(8,128)(2,1)S(1)}, bf16[64,2048]{1,0:T(8,128)(2,1)S(1)}, u32[]{:S(2)}, u32[]{:S(2)}) collective-permute-start(bf16[64,2048]{1,0:T(8,128)(2,1)S(1)} %get-tuple-element.35), channel_id=1, source_target_pairs={{0,4},{2,6},{4,0},{6,2},{1,5},{3,7},{5,1},{7,3},{8,12},{10,14},{12... | collective-permute-start | bytes 786440 | tf_op jit(solution)/shard_map/ppermute | solution.py:76
  145.8 14.3 %collective-permute-start.18 = (bf16[64,2048]{1,0:T(8,128)(2,1)S(1)}, bf16[64,2048]{1,0:T(8,128)(2,1)}, u32[]{:S(2)}, u32[]{:S(2)}) collective-permute-start(bf16[64,2048]{1,0:T(8,128)(2,1)S(1)} %get-tuple-element.33), channel_id=1, source_target_pairs={{0,2},{2,4},{4,6},{6,0},{1,3},{3,5},{5,7},{7,1},{8,10},{10,12},{12... | collective-permute-start | bytes 786440 | tf_op jit(solution)/shard_map/ppermute | solution.py:76
  183.6 35.6 %collective-permute-start.31 = (bf16[2048,448]{0,1:T(8,128)(2,1)}, bf16[2048,448]{0,1:T(8,128)(2,1)}, u32[]{:S(2)}, u32[]{:S(2)}) collective-permute-start(bf16[2048,448]{0,1:T(8,128)(2,1)} %param.32), channel_id=1, source_target_pairs={{0,32},{32,0},{1,33},{33,1},{2,34},{34,2},{3,35},{35,3},{4,36},{36... | collective-permute-start | bytes 5505032 | tf_op jit(solution)/shard_map/ppermute | solution.py:212
  188.2 14.9 %collective-permute-start.29 = (bf16[128,2048]{1,0:T(8,128)(2,1)S(1)}, bf16[128,2048]{1,0:T(8,128)(2,1)S(1)}, u32[]{:S(2)}, u32[]{:S(2)}) collective-permute-start(bf16[128,2048]{1,0:T(8,128)(2,1)S(1)} %maximum_select_fusion.1), channel_id=1, source_target_pairs={{0,6},{2,0},{4,2},{6,4},{1,7},{3,1},{5,3},{7,5},{8,14},{10,8},{12,... | collective-permute-start | bytes 1572872 | tf_op jit(solution)/shard_map/ppermute | solution.py:62
  190.0 16.3 %collective-permute-start.28 = (bf16[128,2048]{1,0:T(8,128)(2,1)S(1)}, bf16[128,2048]{1,0:T(8,128)(2,1)S(1)}, u32[]{:S(2)}, u32[]{:S(2)}) collective-permute-start(bf16[128,2048]{1,0:T(8,128)(2,1)S(1)} %maximum_select_fusion.1), channel_id=1, source_target_pairs={{0,4},{2,6},{4,0},{6,2},{1,5},{3,7},{5,1},{7,3},{8,12},{10,14},{12... | collective-permute-start | bytes 1572872 | tf_op jit(solution)/shard_map/ppermute | solution.py:62
  190.1 22.1 %collective-permute-start.27 = (bf16[128,2048]{1,0:T(8,128)(2,1)S(1)}, bf16[128,2048]{1,0:T(8,128)(2,1)S(1)}, u32[]{:S(2)}, u32[]{:S(2)}) collective-permute-start(bf16[128,2048]{1,0:T(8,128)(2,1)S(1)} %maximum_select_fusion.1), channel_id=1, source_target_pairs={{0,2},{2,4},{4,6},{6,0},{1,3},{3,5},{5,7},{7,1},{8,10},{10,12},{12... | collective-permute-start | bytes 1572872 | tf_op jit(solution)/shard_map/ppermute | solution.py:62
  191.0 30.9 %collective-permute-start.30 = (bf16[2048,448]{0,1:T(8,128)(2,1)}, bf16[2048,448]{0,1:T(8,128)(2,1)}, u32[]{:S(2)}, u32[]{:S(2)}) collective-permute-start(bf16[2048,448]{0,1:T(8,128)(2,1)} %param.31), channel_id=1, source_target_pairs={{0,32},{32,0},{1,33},{33,1},{2,34},{34,2},{3,35},{35,3},{4,36},{36... | collective-permute-start | bytes 5505032 | tf_op jit(solution)/shard_map/ppermute | solution.py:211
  224.8 13.5 %collective-permute-start.34 = (bf16[128,1792]{0,1:T(8,128)(2,1)S(1)}, bf16[128,1792]{0,1:T(8,128)(2,1)S(1)}, u32[]{:S(2)}, u32[]{:S(2)}) collective-permute-start(bf16[128,1792]{0,1:T(8,128)(2,1)S(1)} %get-tuple-element.25), channel_id=1, source_target_pairs={{0,24},{8,0},{16,8},{24,16},{1,25},{9,1},{17,9},{25,17},{2,26},{10... | collective-permute-start | bytes 1376264 | tf_op jit(solution)/shard_map/ppermute | solution.py:76
  226.4 14.9 %collective-permute-start.33 = (bf16[128,1792]{0,1:T(8,128)(2,1)S(1)}, bf16[128,1792]{0,1:T(8,128)(2,1)S(1)}, u32[]{:S(2)}, u32[]{:S(2)}) collective-permute-start(bf16[128,1792]{0,1:T(8,128)(2,1)S(1)} %get-tuple-element.26), channel_id=1, source_target_pairs={{0,16},{8,24},{16,0},{24,8},{1,17},{9,25},{17,1},{25,9},{2,18},{10... | collective-permute-start | bytes 1376264 | tf_op jit(solution)/shard_map/ppermute | solution.py:76
  227.5 22.1 %collective-permute-start.32 = (bf16[128,1792]{0,1:T(8,128)(2,1)S(1)}, bf16[128,1792]{0,1:T(8,128)(2,1)S(1)}, u32[]{:S(2)}, u32[]{:S(2)}) collective-permute-start(bf16[128,1792]{0,1:T(8,128)(2,1)S(1)} %get-tuple-element.24), channel_id=1, source_target_pairs={{0,8},{8,16},{16,24},{24,0},{1,9},{9,17},{17,25},{25,1},{2,10},{10... | collective-permute-start | bytes 1376264 | tf_op jit(solution)/shard_map/ppermute | solution.py:76
  227.5 40.8 %collective-permute-start.38 = (bf16[448,2048]{1,0:T(8,128)(2,1)}, bf16[448,2048]{1,0:T(8,128)(2,1)}, u32[]{:S(2)}, u32[]{:S(2)}) collective-permute-start(bf16[448,2048]{1,0:T(8,128)(2,1)} %param.33), channel_id=1, source_target_pairs={{0,32},{32,0},{1,33},{33,1},{2,34},{34,2},{3,35},{35,3},{4,36},{36... | collective-permute-start | bytes 5505032 | tf_op jit(solution)/shard_map/ppermute | solution.py:213
  250.6 10.0 %collective-permute-start.36 = (bf16[128,896]{0,1:T(8,128)(2,1)S(1)}, bf16[128,896]{0,1:T(8,128)(2,1)S(1)}, u32[]{:S(2)}, u32[]{:S(2)}) collective-permute-start(bf16[128,896]{0,1:T(8,128)(2,1)S(1)} %fusion.48), channel_id=1, source_target_pairs={{0,16},{8,24},{16,0},{24,8},{1,17},{9,25},{17,1},{25,9},{2,18},{10... | collective-permute-start | bytes 688136 | tf_op jit(solution)/shard_map/ppermute | solution.py:62
  252.0 12.1 %collective-permute-start.35 = (bf16[128,896]{0,1:T(8,128)(2,1)S(1)}, bf16[128,896]{0,1:T(8,128)(2,1)S(1)}, u32[]{:S(2)}, u32[]{:S(2)}) collective-permute-start(bf16[128,896]{0,1:T(8,128)(2,1)S(1)} %fusion.48), channel_id=1, source_target_pairs={{0,8},{8,16},{16,24},{24,0},{1,9},{9,17},{17,25},{25,1},{2,10},{10... | collective-permute-start | bytes 688136 | tf_op jit(solution)/shard_map/ppermute | solution.py:62
  273.6 15.1 %collective-permute-start.41 = (bf16[128,2048]{1,0:T(8,128)(2,1)}, bf16[128,2048]{1,0:T(8,128)(2,1)}, u32[]{:S(2)}, u32[]{:S(2)}) collective-permute-start(bf16[128,2048]{1,0:T(8,128)(2,1)} %get-tuple-element.22), channel_id=1, source_target_pairs={{0,6},{2,0},{4,2},{6,4},{1,7},{3,1},{5,3},{7,5},{8,14},{10,8},{12,... | collective-permute-start | bytes 1572872 | tf_op jit(solution)/shard_map/ppermute | solution.py:76
  273.6 16.7 %collective-permute-start.40 = (bf16[128,2048]{1,0:T(8,128)(2,1)}, bf16[128,2048]{1,0:T(8,128)(2,1)}, u32[]{:S(2)}, u32[]{:S(2)}) collective-permute-start(bf16[128,2048]{1,0:T(8,128)(2,1)} %get-tuple-element.23), channel_id=1, source_target_pairs={{0,4},{2,6},{4,0},{6,2},{1,5},{3,7},{5,1},{7,3},{8,12},{10,14},{12... | collective-permute-start | bytes 1572872 | tf_op jit(solution)/shard_map/ppermute | solution.py:76
  273.9 26.6 %collective-permute-start.39 = (bf16[128,2048]{1,0:T(8,128)(2,1)S(1)}, bf16[128,2048]{1,0:T(8,128)(2,1)}, u32[]{:S(2)}, u32[]{:S(2)}) collective-permute-start(bf16[128,2048]{1,0:T(8,128)(2,1)S(1)} %get-tuple-element.21), channel_id=1, source_target_pairs={{0,2},{2,4},{4,6},{6,0},{1,3},{3,5},{5,7},{7,1},{8,10},{10,12},{12... | collective-permute-start | bytes 1572872 | tf_op jit(solution)/shard_map/ppermute | solution.py:76
  302.4 9.8 %collective-permute-start.42 = (bf16[64,2048]{1,0:T(8,128)(2,1)S(1)}, bf16[64,2048]{1,0:T(8,128)(2,1)S(1)}, u32[]{:S(2)}, u32[]{:S(2)}) collective-permute-start(bf16[64,2048]{1,0:T(8,128)(2,1)S(1)} %dynamic-slice_bitcast_fusion.9), channel_id=1, source_target_pairs={{0,64},{64,0},{1,65},{65,1},{2,66},{66,2},{3,67},{67,3},{4,68},{68... | collective-permute-start | bytes 786440 | tf_op jit(solution)/shard_map/ppermute | solution.py:52
  (35 other events, 318.3 us)

commit v2 on v0

--- a/solution.py
+++ b/solution.py
@@ -73,6 +73,26 @@
     for shift in range(1, size):
         pairs = [(i, (i + shift) % size) for i in range(size)]
         outgoing = lax.dynamic_index_in_dim(blocks, (index + shift) % size, 0, keepdims=False)
+        total = total + lax.ppermute(outgoing, axis, pairs).astype(jnp.float32)
+    return total
+
+
+def ring_gather_relative(part, axis):
+    size = lax.axis_size(axis)
+    pieces = [part]
+    for shift in range(1, size):
+        pairs = [(i, (i + shift) % size) for i in range(size)]
+        pieces.append(lax.ppermute(part, axis, pairs))
+    return jnp.concatenate(pieces, axis=0)
+
+
+def ring_reduce_relative(rows, axis):
+    size = lax.axis_size(axis)
+    blocks = rows.reshape((size, rows.shape[0] // size) + rows.shape[1:])
+    total = blocks[0].astype(jnp.float32)
+    for shift in range(1, size):
+        pairs = [(i, (i + shift) % size) for i in range(size)]
+        outgoing = blocks[(size - shift) % size]
         total = total + lax.ppermute(outgoing, axis, pairs).astype(jnp.float32)
     return total
 
@@ -212,7 +232,7 @@
     up_both = jnp.concatenate([w_up, lax.ppermute(w_up, "core", swap)], axis=1)
     down_both = jnp.concatenate([w_down, lax.ppermute(w_down, "core", swap)], axis=0)
     normed_row = pair_gather(pair_gather(normed_own, "xlo"), "hi")
-    normed_half = ring_gather(normed_row, "z")
+    normed_half = ring_gather_relative(normed_row, "z")
     hidden_units = gate_both.shape[1]
     part_gate = jnp.dot(normed_half, gate_both, preferred_element_type=jnp.float32)
     part_upward = jnp.dot(normed_half, up_both, preferred_element_type=jnp.float32)
@@ -223,7 +243,7 @@
     act = (jax.nn.silu(gate) * upward).astype(jnp.bfloat16)
     act_all = ring_gather(act, "grp")
     down = jnp.dot(act_all, down_both, preferred_element_type=jnp.float32)
-    returned = ring_reduce(down.astype(jnp.bfloat16), "z").astype(jnp.bfloat16)
+    returned = ring_reduce_relative(down.astype(jnp.bfloat16), "z").astype(jnp.bfloat16)
     returned = pair_reduce(pair_reduce(returned, "hi").astype(jnp.bfloat16), "xlo")
     return (middle_float + returned.astype(jnp.float32)).astype(jnp.bfloat16)
 

time: 322 us -> 320 us (level)
  local copies, waits for them, and re-layouts: 40.6 us -> 25.7 us
  waiting for transfers between devices: 154 us -> 168 us
    ppermute x0 -> x6, waiting for transfers between devices: none -> 45.6 us  [the longest x3 24.1 us: ring_reduce_relative(): total = total + lax.ppermute(outgoing, axis, pairs).astype(jnp.float32)]
    ppermute x15 -> x12, waiting for transfers between devices: 88.1 us -> 63.6 us  [ring_reduce(): total = total + lax.ppermute(outgoing, axis, pairs).astype(jnp.float32)]
    ppermute x2 -> x0, local copies, waits for them, and re-layouts: 7.69 us -> none  [the longest x1 3.87 us: body(): lax.ppermute(w_gate, 'core', swap)]
    ppermute x21 -> x18, waiting for transfers between devices: 42.2 us -> 35.3 us  [ring_gather(): pieces.append(lax.ppermute(part, axis, pairs))]
    unnamed x38 -> x32, local copies, waits for them, and re-layouts: 8.02 us -> 2.62 us
    ppermute x0 -> x6, starting transfers between devices: none -> 4.38 us  [the longest x3 2.36 us: ring_gather_relative(): pieces.append(lax.ppermute(part, axis, pairs))]
    ppermute x21 -> x18, starting transfers between devices: 24.1 us -> 20.8 us  [ring_gather(): pieces.append(lax.ppermute(part, axis, pairs))]
    gather x7 -> x6, local copies, waits for them, and re-layouts: 6.5 us -> 4.44 us  [ring_gather(): return stacked[order].reshape((size * part.shape[0],) + part.shape[1:])]
  transfers between devices with their start and end apart: 44 -> 44, of which waited for: 35 -> 35; matrix products, arithmetic and copies ran while one was open for 11% -> 6% of each run, Pallas kernels for 0% -> 0%
where the time goes in v2:
time: 320 us; the launch traced here: 314 us
  waiting for transfers between devices  168 us (52%)
  matrix products  56.9 us (18%)
  starting transfers between devices  48.8 us (15%)
  local copies, waits for them, and re-layouts  25.7 us (8%)
  other arithmetic  13.5 us (4%)
    ppermute x12, waiting for transfers between devices, ring_reduce(): total = total + lax.ppermute(outgoing, axis, pairs).astype(jnp.float32)  63.6 us
    ppermute x18, waiting for transfers between devices, ring_gather(): pieces.append(lax.ppermute(part, axis, pairs))  35.3 us
    ppermute x3, waiting for transfers between devices, ring_reduce_relative(): total = total + lax.ppermute(outgoing, axis, pairs).astype(jnp.float32)  24.1 us
    ppermute x3, waiting for transfers between devices, ring_gather_relative(): pieces.append(lax.ppermute(part, axis, pairs))  21.5 us
    ppermute x18, starting transfers between devices, ring_gather(): pieces.append(lax.ppermute(part, axis, pairs))  20.8 us
    ppermute x3, waiting for transfers between devices, pair_reduce(): other = lax.ppermute(other.astype(jnp.bfloat16), axis, swap)  15.7 us
    ppermute x12, starting transfers between devices, ring_reduce(): total = total + lax.ppermute(outgoing, axis, pairs).astype(jnp.float32)  15.6 us
    dot_general x1, matrix products, body(): jnp.einsum('pskgj,pjkd->pskgd', pre_weights, pre_value_ext, preferred_ele...  15.1 us
  transfers between devices with their start and end apart: 44, of which 35 were waited for; matrix products, arithmetic and copies ran while one was open for 6% of the time, Pallas kernels for 0%

profile of v2, /device:TPU:0, one launch (start us, length us, event | category | flops | bytes accessed | tf_op | source)
XLA Modules:
  0.0 313.9 jit_solution(5228968427481418318)
XLA Ops:
  20.3 11.4 %collective-permute-done.5 = f32[64,1280]{1,0:T(8,128)S(1)} collective-permute-done((f32[64,1280]{1,0:T(8,128)S(1)}, f32[64,1280]{1,0:T(8,128)S(1)}, u32[]{:S(2)}, u32[]{:S(2)}) %collective-permute-start.5) | collective-permute-done | bytes 327712 | tf_op jit(solution)/shard_map/ppermute | solution.py:76
  31.7 3.7 %collective-permute-done.3 = f32[64,1280]{1,0:T(8,128)S(1)} collective-permute-done((f32[64,1280]{1,0:T(8,128)S(1)}, f32[64,1280]{1,0:T(8,128)S(1)}, u32[]{:S(2)}, u32[]{:S(2)}) %collective-permute-start.3) | collective-permute-done | bytes 327712 | tf_op jit(solution)/shard_map/ppermute | solution.py:76
  49.5 13.1 %bitcast_reduce_fusion = (f32[2,128,8]{1,2,0:T(8,128)S(1)}, f32[2,128,8,4096]{3,1,2,0:T(8,128)}) fusion(bf16[2,4096,128]{2,1,0:T(8,128)(2,1)S(1)} %copy-done, bf16[2,128,8,128]{3,2,1,0:T(8,128)(2,1)S(1)} %bitcast.222), kind=kOutput, calls=%fused_computation.12 | convolution fusion | flops 2164258816 | bytes 36184064 | tf_op jit(solution)/shard_map/pskgd,pjkd->pskgj/dot_general | solution.py:164
  63.4 4.5 %fusion.96 = (f32[256,8]{1,0:T(8,128)S(1)}, f32[256,8,64]{2,1,0:T(8,128)S(1)}) fusion(bf16[256,8,128]{2,1,0:T(8,128)(2,1)S(1)} %bitcast.221, bf16[256,64,128]{2,1,0:T(8,128)(2,1)} %param.26, pred[256,64]{1,0:T(8,128)(4,1)S(1)} %broadcast_compare_fusion), kind=kOutput, calls=%fused_computation.182 | convolution fusion | flops 33945600 | bytes 5267456 | tf_op jit(solution)/shard_map/skgd,sjkd->skgj/dot_general | solution.py:171
  79.4 15.1 %fusion.26 = f32[2,128,1,8,256]{4,1,3,0,2:T(8,128)} fusion(f32[2,128,8,4096]{3,1,2,0:T(8,128)} %get-tuple-element.42, f32[2,128,8]{1,2,0:T(8,128)S(1)} %copy.82, bf16[2,4096,1,128]{3,1,0,2:T(8,128)(2,1)} %bitcast.274, bf16[256]{0:T(256)(128)(2,1)S(1)} %pad.52.clone), kind=kOutput, calls=%fused_computation.53 | convolution fusion | flops 4328521728 | bytes 37757440 | tf_op jit(solution)/shard_map/pskgj,pjkd->pskgd/dot_general | solution.py:191
  94.5 4.2 %copy.83 = f32[2,128,1,8,256]{4,3,1,0,2:T(8,128)} copy(f32[2,128,1,8,256]{4,1,3,0,2:T(8,128)} %fusion.26) | data formatting | bytes 4194304 | tf_op jit(solution)/shard_map/pskgj,pjkd->pskgd/transpose | solution.py:191
  98.6 3.7 %gather_fusion.6 = f32[256,8,256]{2,1,0:T(8,128)} fusion(f32[256,8,256]{2,1,0:T(8,128)} %bitcast.216, s32[1024]{0:T(1024)S(1)} %pad_clamp_fusion), kind=kCustom, calls=%fused_computation.6 | custom fusion | bytes 4195328 | tf_op jit(solution)/shard_map/gather | solution.py:194
  114.2 6.6 %collective-permute-done.14 = f32[64,1032]{1,0:T(8,128)S(1)} collective-permute-done((f32[64,1032]{1,0:T(8,128)S(1)}, f32[64,1032]{1,0:T(8,128)S(1)}, u32[]{:S(2)}, u32[]{:S(2)}) %collective-permute-start.14) | collective-permute-done | bytes 264224 | tf_op jit(solution)/shard_map/ppermute | solution.py:76
  123.4 3.7 %collective-permute-done.12 = f32[64,1032]{1,0:T(8,128)S(1)} collective-permute-done((f32[64,1032]{1,0:T(8,128)S(1)}, f32[64,1032]{1,0:T(8,128)S(1)}, u32[]{:S(2)}, u32[]{:S(2)}) %collective-permute-start.12) | collective-permute-done | bytes 264224 | tf_op jit(solution)/shard_map/ppermute | solution.py:76
  141.7 4.1 %collective-permute-start.20 = (bf16[64,2048]{1,0:T(8,128)(2,1)S(1)}, bf16[64,2048]{1,0:T(8,128)(2,1)S(1)}, u32[]{:S(2)}, u32[]{:S(2)}) collective-permute-start(bf16[64,2048]{1,0:T(8,128)(2,1)S(1)} %get-tuple-element.34), channel_id=1, source_target_pairs={{0,6},{2,0},{4,2},{6,4},{1,7},{3,1},{5,3},{7,5},{8,14},{10,8},{12,... | collective-permute-start | bytes 786440 | tf_op jit(solution)/shard_map/ppermute | solution.py:76
  147.1 9.5 %collective-permute-done.20 = bf16[64,2048]{1,0:T(8,128)(2,1)S(1)} collective-permute-done((bf16[64,2048]{1,0:T(8,128)(2,1)S(1)}, bf16[64,2048]{1,0:T(8,128)(2,1)S(1)}, u32[]{:S(2)}, u32[]{:S(2)}) %collective-permute-start.20) | collective-permute-done | bytes 262176 | tf_op jit(solution)/shard_map/ppermute | solution.py:76
  183.6 4.5 %collective-permute-done.26 = bf16[64,2048]{1,0:T(8,128)(2,1)S(1)} collective-permute-done((bf16[64,2048]{1,0:T(8,128)(2,1)S(1)}, bf16[64,2048]{1,0:T(8,128)(2,1)S(1)}, u32[]{:S(2)}, u32[]{:S(2)}) %collective-permute-start.26) | collective-permute-done | bytes 262176 | tf_op jit(solution)/shard_map/ppermute | solution.py:39
  190.6 12.5 %collective-permute-done.29 = bf16[128,2048]{1,0:T(8,128)(2,1)S(1)} collective-permute-done((bf16[128,2048]{1,0:T(8,128)(2,1)S(1)}, bf16[128,2048]{1,0:T(8,128)(2,1)S(1)}, u32[]{:S(2)}, u32[]{:S(2)}) %collective-permute-start.29) | collective-permute-done | bytes 524320 | tf_op jit(solution)/shard_map/ppermute | solution.py:85
  205.4 6.7 %collective-permute-done.27 = bf16[128,2048]{1,0:T(8,128)(2,1)S(1)} collective-permute-done((bf16[128,2048]{1,0:T(8,128)(2,1)S(1)}, bf16[128,2048]{1,0:T(8,128)(2,1)S(1)}, u32[]{:S(2)}, u32[]{:S(2)}) %collective-permute-start.27) | collective-permute-done | bytes 524320 | tf_op jit(solution)/shard_map/ppermute | solution.py:85
  212.1 4.4 %fusion.32 = bf16[512,896]{1,0:T(8,128)(2,1)S(1)} fusion(bf16[2048,448]{0,1:T(8,128)(2,1)} %collective-permute-done.30, bf16[2048,448]{0,1:T(8,128)(2,1)} %param.31, bf16[128,2048]{1,0:T(8,128)(2,1)S(1)} %collective-permute-done.29, bf16[128,2048]{1,0:T(8,128)(2,1)S(1)} %collective-permute-done.28, bf16[128,2048]{1,0:T(8,128)(2,1)S(1)} %collective-permute-done.27, ...), kind=kOutput, calls=%fused_computation.55 | convolution fusion | flops 1895235584 | bytes 6684672 | tf_op jit(solution)/shard_map/dot_general | solution.py:237
  216.6 3.9 %fusion.29 = bf16[512,896]{1,0:T(8,128)(2,1)S(1)} fusion(bf16[2048,448]{0,1:T(8,128)(2,1)} %collective-permute-done.31, bf16[2048,448]{0,1:T(8,128)(2,1)S(1)} %copy-done.11, bf16[128,2048]{1,0:T(8,128)(2,1)S(1)} %collective-permute-done.29, bf16[128,2048]{1,0:T(8,128)(2,1)S(1)} %collective-permute-done.28, ...), kind=kOutput, calls=%fused_computation.54 | convolution fusion | flops 1895235584 | bytes 6684672 | tf_op jit(solution)/shard_map/dot_general | solution.py:238
  223.5 18.8 %collective-permute-done.34 = bf16[128,1792]{1,0:T(8,128)(2,1)S(1)} collective-permute-done((bf16[128,1792]{1,0:T(8,128)(2,1)S(1)}, bf16[128,1792]{1,0:T(8,128)(2,1)S(1)}, u32[]{:S(2)}, u32[]{:S(2)}) %collective-permute-start.34) | collective-permute-done | bytes 458784 | tf_op jit(solution)/shard_map/ppermute | solution.py:76
  242.2 3.7 %collective-permute-done.32 = bf16[128,1792]{1,0:T(8,128)(2,1)S(1)} collective-permute-done((bf16[128,1792]{1,0:T(8,128)(2,1)S(1)}, bf16[128,1792]{1,0:T(8,128)(2,1)S(1)}, u32[]{:S(2)}, u32[]{:S(2)}) %collective-permute-start.32) | collective-permute-done | bytes 458784 | tf_op jit(solution)/shard_map/ppermute | solution.py:76
  249.0 5.8 %collective-permute-done.37 = bf16[128,896]{1,0:T(8,128)(2,1)S(1)} collective-permute-done((bf16[128,896]{1,0:T(8,128)(2,1)S(1)}, bf16[128,896]{1,0:T(8,128)(2,1)S(1)}, u32[]{:S(2)}, u32[]{:S(2)}) %collective-permute-start.37) | collective-permute-done | bytes 229408 | tf_op jit(solution)/shard_map/ppermute | solution.py:62
  262.1 4.7 %fusion.20 = bf16[512,2048]{1,0:T(8,128)(2,1)S(1)} fusion(bf16[512,896]{1,0:T(8,128)(2,1)} %bitcast.239, bf16[448,2048]{1,0:T(8,128)(2,1)} %collective-permute-done.38, bf16[448,2048]{1,0:T(8,128)(2,1)} %param.33), kind=kOutput, calls=%fused_computation.33 | convolution fusion | flops 1887436800 | bytes 6684672 | tf_op jit(solution)/shard_map/dot_general | solution.py:245
  271.4 13.0 %collective-permute-done.41 = bf16[128,2048]{1,0:T(8,128)(2,1)S(1)} collective-permute-done((bf16[128,2048]{1,0:T(8,128)(2,1)}, bf16[128,2048]{1,0:T(8,128)(2,1)S(1)}, u32[]{:S(2)}, u32[]{:S(2)}) %collective-permute-start.41) | collective-permute-done | bytes 524320 | tf_op jit(solution)/shard_map/ppermute | solution.py:96
  286.7 9.5 %collective-permute-done.39 = bf16[128,2048]{1,0:T(8,128)(2,1)} collective-permute-done((bf16[128,2048]{1,0:T(8,128)(2,1)}, bf16[128,2048]{1,0:T(8,128)(2,1)}, u32[]{:S(2)}, u32[]{:S(2)}) %collective-permute-start.39) | collective-permute-done | bytes 524320 | tf_op jit(solution)/shard_map/ppermute | solution.py:96
  299.1 8.7 %collective-permute-done.42 = bf16[64,2048]{1,0:T(8,128)(2,1)S(1)} collective-permute-done((bf16[64,2048]{1,0:T(8,128)(2,1)S(1)}, bf16[64,2048]{1,0:T(8,128)(2,1)S(1)}, u32[]{:S(2)}, u32[]{:S(2)}) %collective-permute-start.42) | collective-permute-done | bytes 262176 | tf_op jit(solution)/shard_map/ppermute | solution.py:52
  308.0 5.0 %collective-permute-done.43 = bf16[32,2048]{1,0:T(8,128)(2,1)S(1)} collective-permute-done((bf16[32,2048]{1,0:T(8,128)(2,1)S(1)}, bf16[32,2048]{1,0:T(8,128)(2,1)S(1)}, u32[]{:S(2)}, u32[]{:S(2)}) %collective-permute-start.43) | collective-permute-done | bytes 131104 | tf_op jit(solution)/shard_map/ppermute | solution.py:52
  (195 shorter events, 132.4 us)
Async XLA Ops:
  16.2 15.5 %collective-permute-start.5 = (f32[64,1280]{1,0:T(8,128)S(1)}, f32[64,1280]{1,0:T(8,128)S(1)}, u32[]{:S(2)}, u32[]{:S(2)}) collective-permute-start(f32[64,1280]{1,0:T(8,128)S(1)} %get-tuple-element.28), channel_id=1, source_target_pairs={{0,24},{8,0},{16,8},{24,16},{1,25},{9,1},{17,9},{25,17},{2,26},{10... | collective-permute-start | bytes 983048 | tf_op jit(solution)/shard_map/ppermute | solution.py:76
  18.5 13.2 %collective-permute-start.4 = (f32[64,1280]{1,0:T(8,128)S(1)}, f32[64,1280]{1,0:T(8,128)S(1)}, u32[]{:S(2)}, u32[]{:S(2)}) collective-permute-start(f32[64,1280]{1,0:T(8,128)S(1)} %get-tuple-element.29), channel_id=1, source_target_pairs={{0,16},{8,24},{16,0},{24,8},{1,17},{9,25},{17,1},{25,9},{2,18},{10... | collective-permute-start | bytes 983048 | tf_op jit(solution)/shard_map/ppermute | solution.py:76
  20.2 15.2 %collective-permute-start.3 = (f32[64,1280]{1,0:T(8,128)S(1)}, f32[64,1280]{1,0:T(8,128)S(1)}, u32[]{:S(2)}, u32[]{:S(2)}) collective-permute-start(f32[64,1280]{1,0:T(8,128)S(1)} %get-tuple-element.27), channel_id=1, source_target_pairs={{0,8},{8,16},{16,24},{24,0},{1,9},{9,17},{17,25},{25,1},{2,10},{10... | collective-permute-start | bytes 983048 | tf_op jit(solution)/shard_map/ppermute | solution.py:76
  110.8 10.0 %collective-permute-start.14 = (f32[64,1032]{1,0:T(8,128)S(1)}, f32[64,1032]{1,0:T(8,128)S(1)}, u32[]{:S(2)}, u32[]{:S(2)}) collective-permute-start(f32[64,1032]{1,0:T(8,128)S(1)} %get-tuple-element.32), channel_id=1, source_target_pairs={{0,24},{8,0},{16,8},{24,16},{1,25},{9,1},{17,9},{25,17},{2,26},{10... | collective-permute-start | bytes 792584 | tf_op jit(solution)/shard_map/ppermute | solution.py:76
  112.0 11.4 %collective-permute-start.13 = (f32[64,1032]{1,0:T(8,128)S(1)}, f32[64,1032]{1,0:T(8,128)S(1)}, u32[]{:S(2)}, u32[]{:S(2)}) collective-permute-start(f32[64,1032]{1,0:T(8,128)S(1)} %get-tuple-element.31), channel_id=1, source_target_pairs={{0,16},{8,24},{16,0},{24,8},{1,17},{9,25},{17,1},{25,9},{2,18},{10... | collective-permute-start | bytes 792584 | tf_op jit(solution)/shard_map/ppermute | solution.py:76
  113.3 13.9 %collective-permute-start.12 = (f32[64,1032]{1,0:T(8,128)S(1)}, f32[64,1032]{1,0:T(8,128)S(1)}, u32[]{:S(2)}, u32[]{:S(2)}) collective-permute-start(f32[64,1032]{1,0:T(8,128)S(1)} %get-tuple-element.30), channel_id=1, source_target_pairs={{0,8},{8,16},{16,24},{24,0},{1,9},{9,17},{17,25},{25,1},{2,10},{10... | collective-permute-start | bytes 792584 | tf_op jit(solution)/shard_map/ppermute | solution.py:76
  141.7 14.9 %collective-permute-start.20 = (bf16[64,2048]{1,0:T(8,128)(2,1)S(1)}, bf16[64,2048]{1,0:T(8,128)(2,1)S(1)}, u32[]{:S(2)}, u32[]{:S(2)}) collective-permute-start(bf16[64,2048]{1,0:T(8,128)(2,1)S(1)} %get-tuple-element.34), channel_id=1, source_target_pairs={{0,6},{2,0},{4,2},{6,4},{1,7},{3,1},{5,3},{7,5},{8,14},{10,8},{12,... | collective-permute-start | bytes 786440 | tf_op jit(solution)/shard_map/ppermute | solution.py:76
  145.8 10.8 %collective-permute-start.19 = (bf16[64,2048]{1,0:T(8,128)(2,1)S(1)}, bf16[64,2048]{1,0:T(8,128)(2,1)S(1)}, u32[]{:S(2)}, u32[]{:S(2)}) collective-permute-start(bf16[64,2048]{1,0:T(8,128)(2,1)S(1)} %get-tuple-element.35), channel_id=1, source_target_pairs={{0,4},{2,6},{4,0},{6,2},{1,5},{3,7},{5,1},{7,3},{8,12},{10,14},{12... | collective-permute-start | bytes 786440 | tf_op jit(solution)/shard_map/ppermute | solution.py:76
  145.8 14.3 %collective-permute-start.18 = (bf16[64,2048]{1,0:T(8,128)(2,1)S(1)}, bf16[64,2048]{1,0:T(8,128)(2,1)}, u32[]{:S(2)}, u32[]{:S(2)}) collective-permute-start(bf16[64,2048]{1,0:T(8,128)(2,1)S(1)} %get-tuple-element.33), channel_id=1, source_target_pairs={{0,2},{2,4},{4,6},{6,0},{1,3},{3,5},{5,7},{7,1},{8,10},{10,12},{12... | collective-permute-start | bytes 786440 | tf_op jit(solution)/shard_map/ppermute | solution.py:76
  163.0 27.5 %collective-permute-start.30 = (bf16[2048,448]{0,1:T(8,128)(2,1)}, bf16[2048,448]{0,1:T(8,128)(2,1)}, u32[]{:S(2)}, u32[]{:S(2)}) collective-permute-start(bf16[2048,448]{0,1:T(8,128)(2,1)} %param.31), channel_id=1, source_target_pairs={{0,32},{32,0},{1,33},{33,1},{2,34},{34,2},{3,35},{35,3},{4,36},{36... | collective-permute-start | bytes 5505032 | tf_op jit(solution)/shard_map/ppermute | solution.py:231
  176.6 39.9 %collective-permute-start.31 = (bf16[2048,448]{0,1:T(8,128)(2,1)}, bf16[2048,448]{0,1:T(8,128)(2,1)}, u32[]{:S(2)}, u32[]{:S(2)}) collective-permute-start(bf16[2048,448]{0,1:T(8,128)(2,1)} %param.32), channel_id=1, source_target_pairs={{0,32},{32,0},{1,33},{33,1},{2,34},{34,2},{3,35},{35,3},{4,36},{36... | collective-permute-start | bytes 5505032 | tf_op jit(solution)/shard_map/ppermute | solution.py:232
  188.2 14.9 %collective-permute-start.29 = (bf16[128,2048]{1,0:T(8,128)(2,1)S(1)}, bf16[128,2048]{1,0:T(8,128)(2,1)S(1)}, u32[]{:S(2)}, u32[]{:S(2)}) collective-permute-start(bf16[128,2048]{1,0:T(8,128)(2,1)S(1)} %maximum_select_fusion), channel_id=1, source_target_pairs={{0,6},{2,0},{4,2},{6,4},{1,7},{3,1},{5,3},{7,5},{8,14},{10,8},{12,... | collective-permute-start | bytes 1572872 | tf_op jit(solution)/shard_map/ppermute | solution.py:85
  189.1 16.3 %collective-permute-start.28 = (bf16[128,2048]{1,0:T(8,128)(2,1)S(1)}, bf16[128,2048]{1,0:T(8,128)(2,1)S(1)}, u32[]{:S(2)}, u32[]{:S(2)}) collective-permute-start(bf16[128,2048]{1,0:T(8,128)(2,1)S(1)} %maximum_select_fusion), channel_id=1, source_target_pairs={{0,4},{2,6},{4,0},{6,2},{1,5},{3,7},{5,1},{7,3},{8,12},{10,14},{12... | collective-permute-start | bytes 1572872 | tf_op jit(solution)/shard_map/ppermute | solution.py:85
  189.4 22.7 %collective-permute-start.27 = (bf16[128,2048]{1,0:T(8,128)(2,1)S(1)}, bf16[128,2048]{1,0:T(8,128)(2,1)S(1)}, u32[]{:S(2)}, u32[]{:S(2)}) collective-permute-start(bf16[128,2048]{1,0:T(8,128)(2,1)S(1)} %maximum_select_fusion), channel_id=1, source_target_pairs={{0,2},{2,4},{4,6},{6,0},{1,3},{3,5},{5,7},{7,1},{8,10},{10,12},{12... | collective-permute-start | bytes 1572872 | tf_op jit(solution)/shard_map/ppermute | solution.py:85
  190.6 71.5 %collective-permute-start.38 = (bf16[448,2048]{1,0:T(8,128)(2,1)}, bf16[448,2048]{1,0:T(8,128)(2,1)}, u32[]{:S(2)}, u32[]{:S(2)}) collective-permute-start(bf16[448,2048]{1,0:T(8,128)(2,1)} %param.33), channel_id=1, source_target_pairs={{0,32},{32,0},{1,33},{33,1},{2,34},{34,2},{3,35},{35,3},{4,36},{36... | collective-permute-start | bytes 5505032 | tf_op jit(solution)/shard_map/ppermute | solution.py:233
  220.6 21.7 %collective-permute-start.34 = (bf16[128,1792]{1,0:T(8,128)(2,1)S(1)}, bf16[128,1792]{1,0:T(8,128)(2,1)S(1)}, u32[]{:S(2)}, u32[]{:S(2)}) collective-permute-start(bf16[128,1792]{1,0:T(8,128)(2,1)S(1)} %get-tuple-element.26), channel_id=1, source_target_pairs={{0,24},{8,0},{16,8},{24,16},{1,25},{9,1},{17,9},{25,17},{2,26},{10... | collective-permute-start | bytes 1376264 | tf_op jit(solution)/shard_map/ppermute | solution.py:76
  222.4 19.8 %collective-permute-start.33 = (bf16[128,1792]{1,0:T(8,128)(2,1)S(1)}, bf16[128,1792]{1,0:T(8,128)(2,1)S(1)}, u32[]{:S(2)}, u32[]{:S(2)}) collective-permute-start(bf16[128,1792]{1,0:T(8,128)(2,1)S(1)} %get-tuple-element.25), channel_id=1, source_target_pairs={{0,16},{8,24},{16,0},{24,8},{1,17},{9,25},{17,1},{25,9},{2,18},{10... | collective-permute-start | bytes 1376264 | tf_op jit(solution)/shard_map/ppermute | solution.py:76
  223.3 22.6 %collective-permute-start.32 = (bf16[128,1792]{1,0:T(8,128)(2,1)S(1)}, bf16[128,1792]{1,0:T(8,128)(2,1)S(1)}, u32[]{:S(2)}, u32[]{:S(2)}) collective-permute-start(bf16[128,1792]{1,0:T(8,128)(2,1)S(1)} %get-tuple-element.24), channel_id=1, source_target_pairs={{0,8},{8,16},{16,24},{24,0},{1,9},{9,17},{17,25},{25,1},{2,10},{10... | collective-permute-start | bytes 1376264 | tf_op jit(solution)/shard_map/ppermute | solution.py:76
  247.0 10.0 %collective-permute-start.36 = (bf16[128,896]{1,0:T(8,128)(2,1)S(1)}, bf16[128,896]{1,0:T(8,128)(2,1)S(1)}, u32[]{:S(2)}, u32[]{:S(2)}) collective-permute-start(bf16[128,896]{1,0:T(8,128)(2,1)S(1)} %fusion.51), channel_id=1, source_target_pairs={{0,16},{8,24},{16,0},{24,8},{1,17},{9,25},{17,1},{25,9},{2,18},{10... | collective-permute-start | bytes 688136 | tf_op jit(solution)/shard_map/ppermute | solution.py:62
  247.9 12.5 %collective-permute-start.35 = (bf16[128,896]{1,0:T(8,128)(2,1)S(1)}, bf16[128,896]{1,0:T(8,128)(2,1)S(1)}, u32[]{:S(2)}, u32[]{:S(2)}) collective-permute-start(bf16[128,896]{1,0:T(8,128)(2,1)S(1)} %fusion.51), channel_id=1, source_target_pairs={{0,8},{8,16},{16,24},{24,0},{1,9},{9,17},{17,25},{25,1},{2,10},{10... | collective-permute-start | bytes 688136 | tf_op jit(solution)/shard_map/ppermute | solution.py:62
  269.4 15.0 %collective-permute-start.41 = (bf16[128,2048]{1,0:T(8,128)(2,1)}, bf16[128,2048]{1,0:T(8,128)(2,1)S(1)}, u32[]{:S(2)}, u32[]{:S(2)}) collective-permute-start(bf16[128,2048]{1,0:T(8,128)(2,1)} %get-tuple-element.22), channel_id=1, source_target_pairs={{0,6},{2,0},{4,2},{6,4},{1,7},{3,1},{5,3},{7,5},{8,14},{10,8},{12,... | collective-permute-start | bytes 1572872 | tf_op jit(solution)/shard_map/ppermute | solution.py:96
  269.4 16.6 %collective-permute-start.40 = (bf16[128,2048]{1,0:T(8,128)(2,1)}, bf16[128,2048]{1,0:T(8,128)(2,1)S(1)}, u32[]{:S(2)}, u32[]{:S(2)}) collective-permute-start(bf16[128,2048]{1,0:T(8,128)(2,1)} %get-tuple-element.23), channel_id=1, source_target_pairs={{0,4},{2,6},{4,0},{6,2},{1,5},{3,7},{5,1},{7,3},{8,12},{10,14},{12... | collective-permute-start | bytes 1572872 | tf_op jit(solution)/shard_map/ppermute | solution.py:96
  269.9 26.4 %collective-permute-start.39 = (bf16[128,2048]{1,0:T(8,128)(2,1)}, bf16[128,2048]{1,0:T(8,128)(2,1)}, u32[]{:S(2)}, u32[]{:S(2)}) collective-permute-start(bf16[128,2048]{1,0:T(8,128)(2,1)} %get-tuple-element.21), channel_id=1, source_target_pairs={{0,2},{2,4},{4,6},{6,0},{1,3},{3,5},{5,7},{7,1},{8,10},{10,12},{12... | collective-permute-start | bytes 1572872 | tf_op jit(solution)/shard_map/ppermute | solution.py:96
  298.0 9.8 %collective-permute-start.42 = (bf16[64,2048]{1,0:T(8,128)(2,1)S(1)}, bf16[64,2048]{1,0:T(8,128)(2,1)S(1)}, u32[]{:S(2)}, u32[]{:S(2)}) collective-permute-start(bf16[64,2048]{1,0:T(8,128)(2,1)S(1)} %dynamic-slice_bitcast_fusion.3), channel_id=1, source_target_pairs={{0,64},{64,0},{1,65},{65,1},{2,66},{66,2},{3,67},{67,3},{4,68},{68... | collective-permute-start | bytes 786440 | tf_op jit(solution)/shard_map/ppermute | solution.py:52
  (35 other events, 339.8 us)
